TPU v7x, 128 devices: a whole 4x4x4 slice. The times are simulated.
128 devices in a mesh: row: 8 (over x_lo, z), col: 16 (over y, x_hi, core).
Axes of the slice: x: 4 (x_hi: 2, x_lo: 2; x = x_hi * 2 + x_lo), y: 4, z: 4, core: 2. Of those that a mesh axis runs over, the one named last changes fastest.
Arguments:
- adjusted_rows: bfloat16 [8192, 29568], P(('row', 'col')), may hold values from -5 to 5
- base_weight: bfloat16 [8192, 29568], P('row', 'col'), may hold values from -5 to 5
- range_test: bfloat16 [29568, 384], P('col'), may hold values from -0.03125 to 0.03125
- corange_test: bfloat16 [384, 8192], P(None, 'row'), may hold values from -0.0625 to 0.0625
- core_left: bfloat16 [768, 8192], P(None, 'row'), may hold values from -0.0625 to 0.0625
- core_right: bfloat16 [768, 29568], P(None, 'col'), may hold values from -1 to 1
Outputs:
- range_sketch: float32 [8192, 384], P('row')
- corange_sketch: float32 [384, 29568], P(None, 'col')
- core_solution: float32 [384, 768], P(None, 'col')
All inputs are finite; a program needn't handle non-finite values.
Results may differ from a plain program's by a relative error of at most 0.0066.
Values may be sent and summed in bfloat16 or wider, within the bound.
No kernel may reach another device: no remote copies, remote signals or barrier semaphores. Data moves between devices by JAX's collectives and lax.ppermute only.
A program may use at most 128 MiB of HBM per device.

v0:
```python
import jax
import jax.numpy as jnp
from jax import lax
from jax.sharding import PartitionSpec as P

S = 768


def scatter_sum(part, axis, groups):
    rows = part.shape[0] // groups
    got = lax.all_to_all(part, axis, split_axis=0, concat_axis=0, tiled=True)
    return got.reshape(groups, rows, *part.shape[1:]).sum(axis=0)


def gather_rows(chunk, axis, groups):
    tiled = jnp.broadcast_to(chunk[None], (groups, *chunk.shape)).reshape(
        groups * chunk.shape[0], *chunk.shape[1:]
    )
    return lax.all_to_all(tiled, axis, split_axis=0, concat_axis=0, tiled=True)


def dot_hi(a, b):
    return jnp.dot(a, b, precision=lax.Precision.HIGHEST)


def cholesky_solve(gram, rhs, size=128):
    count = gram.shape[0] // size
    gram = (gram + gram.T) * 0.5
    block = lambda i, j: gram[i * size:(i + 1) * size, j * size:(j + 1) * size]
    eye = jnp.eye(size, dtype=gram.dtype)
    low = {}
    inverse = []
    for j in range(count):
        a = block(j, j)
        for m in range(j):
            a = a - dot_hi(low[j, m], low[j, m].T)
        low[j, j] = lax.linalg.cholesky(a, symmetrize_input=False)
        inverse.append(lax.linalg.triangular_solve(low[j, j], eye, left_side=True, lower=True))
        for i in range(j + 1, count):
            a = block(i, j)
            for m in range(j):
                a = a - dot_hi(low[i, m], low[j, m].T)
            low[i, j] = dot_hi(a, inverse[j].T)
    halfway = []
    for i in range(count):
        r = rhs[i * size:(i + 1) * size]
        for m in range(i):
            r = r - dot_hi(low[i, m], halfway[m])
        halfway.append(dot_hi(inverse[i], r))
    result = [None] * count
    for i in reversed(range(count)):
        r = halfway[i]
        for m in range(i + 1, count):
            r = r - dot_hi(low[m, i].T, result[m])
        result[i] = dot_hi(inverse[i].T, r)
    return jnp.concatenate(result, axis=0)


def local(adjusted_rows, base_weight, range_test, corange_test, core_left, core_right):
    highest = lax.Precision.HIGHEST
    ncol = lax.axis_size("col")
    nrow = lax.axis_size("row")
    height, width = adjusted_rows.shape[0], adjusted_rows.shape[1] // ncol
    by_target = adjusted_rows.reshape(height, ncol, width).transpose(1, 0, 2)
    adjusted_block = lax.all_to_all(by_target, "col", split_axis=0, concat_axis=0, tiled=True)
    adjusted_block = adjusted_block.reshape(ncol * height, width)
    difference = (adjusted_block.astype(jnp.float32) - base_weight.astype(jnp.float32)).astype(
        jnp.bfloat16
    )
    left_product = jnp.dot(core_left, difference, preferred_element_type=jnp.float32)
    partial_value = jnp.dot(left_product, core_right.astype(jnp.float32).T, precision=highest)
    own_columns = lax.psum_scatter(partial_value, "col", scatter_dimension=1, tiled=True)
    corange_part = jnp.dot(corange_test, difference, preferred_element_type=jnp.float32)
    corange_sketch = lax.psum(corange_part, "row")
    range_part = jnp.dot(difference, range_test, preferred_element_type=jnp.float32)
    left_float = core_left.astype(jnp.float32)
    projected_part = jnp.dot(left_float, range_part, precision=highest)
    every = ("row", "col")
    projected = gather_rows(scatter_sum(projected_part, every, nrow * ncol), every, nrow * ncol)
    projected, range_part, own_columns = lax.optimization_barrier(
        (projected, range_part, own_columns)
    )
    own_columns = gather_rows(scatter_sum(own_columns, "row", nrow), "row", nrow)
    range_sketch = gather_rows(scatter_sum(range_part, "col", ncol), "col", ncol)
    gram_matrix = jnp.dot(projected.T, projected, precision=highest)
    right_hand = jnp.dot(projected.T, own_columns, precision=highest)
    core_solution = cholesky_solve(gram_matrix, right_hand)
    return (range_sketch, corange_sketch, core_solution)


def solution(mesh):
    in_specs = (
        P(("row", "col"), None),
        P("row", "col"),
        P("col", None),
        P(None, "row"),
        P(None, "row"),
        P(None, "col"),
    )
    out_specs = (P("row", None), P(None, "col"), P(None, "col"))
    return jax.shard_map(local, mesh=mesh, in_specs=in_specs, out_specs=out_specs, check_vma=False)
```

profile of v0, /device:TPU:0, one launch (start us, length us, event | category | flops | bytes accessed | tf_op | source)
XLA Modules:
  0.0 342.0 jit_solution(6075751329435946060)
XLA Ops:
  8.0 8.6 %reshape.49 = bf16[64,16,1848]{2,1,0:T(8,128)(2,1)} reshape(bf16[64,29568]{1,0:T(8,128)(2,1)} %param.9) | data formatting | bytes 7569408 | tf_op jit(solution)/shard_map/reshape | solution.py:64
  16.6 4.9 %copy.30 = bf16[64,16,1848]{2,0,1:T(8,128)(2,1)} copy(bf16[64,16,1848]{2,1,0:T(8,128)(2,1)} %reshape.49) | data formatting | bytes 7569408 | tf_op jit(solution)/shard_map/reshape | solution.py:64
  21.5 7.2 %all-to-all-start = ((bf16[16,64,1848]{2,1,0:T(8,128)(2,1)}), bf16[16,64,1848]{2,1,0:T(8,128)(2,1)}, u32[]{:S(2)}, u32[]{:S(2)}) async-start(bf16[16,64,1848]{2,1,0:T(8,128)(2,1)} %bitcast.84), calls=%async_computation | async-start | bytes 7864320 | tf_op jit(solution)/shard_map/all_to_all | solution.py:65
  28.7 6.3 %copy.22 = bf16[1024,1848]{1,0:T(8,128)(2,1)} copy(bf16[1024,1848]{0,1:T(8,128)(2,1)} %param.10) | data formatting | bytes 7569408 | tf_op args[1]
  35.1 42.6 %all-to-all-done = bf16[16,64,1848]{2,1,0:T(8,128)(2,1)} async-done(((bf16[16,64,1848]{2,1,0:T(8,128)(2,1)}), bf16[16,64,1848]{2,1,0:T(8,128)(2,1)}, u32[]{:S(2)}, u32[]{:S(2)}) %all-to-all-start) | async-done | bytes 3784736 | tf_op jit(solution)/shard_map/all_to_all | solution.py:65
  77.7 4.4 %fusion = bf16[1024,1848]{1,0:T(8,128)(2,1)S(1)} fusion(bf16[1024,1848]{1,0:T(8,128)(2,1)} %copy.22, bf16[16,64,1848]{2,1,0:T(8,128)(2,1)} %all-to-all-done), kind=kLoop, calls=%fused_computation.1 | loop fusion | flops 7569408 | bytes 11354112 | tf_op jit(solution)/shard_map/convert_element_type | solution.py:67
  85.5 9.7 %fusion.22 = f32[768,768]{0,1:T(8,128)} fusion(f32[1848,768]{1,0:T(8,128)S(1)} %fusion.21, bf16[768,1848]{0,1:T(8,128)(2,1)S(1)} %copy-done), kind=kOutput, calls=%fused_computation.49 | convolution fusion | flops 13079937024 | bytes 10874880 | tf_op jit(solution)/shard_map/dot_general | solution.py:71
  96.5 5.6 %fusion.20 = f32[1024,384]{1,0:T(8,128)} fusion(bf16[1024,1848]{1,0:T(8,128)(2,1)} %copy-done.2, bf16[1848,384]{1,0:T(8,128)(2,1)S(1)} %copy-done.9), kind=kOutput, calls=%fused_computation.47 | convolution fusion | flops 1453326336 | bytes 6776832 | tf_op jit(solution)/shard_map/dot_general | solution.py:75
  102.1 5.3 %convolution_bitcast_fusion.1 = f32[768,384]{0,1:T(8,128)S(1)} fusion(f32[1024,384]{1,0:T(8,128)} %fusion.20, bf16[768,1024]{1,0:T(8,128)(2,1)S(1)} %copy-done.7), kind=kOutput, calls=%fused_computation.4 | convolution fusion | flops 3623878656 | bytes 4325376 | tf_op jit(solution)/shard_map/dot_general | solution.py:77
  109.1 36.7 %all_to_all.59 = f32[128,6,384]{2,1,0:T(8,128)S(1)} all-to-all(f32[128,6,384]{2,1,0:T(8,128)} %all_to_all.40), channel_id=1, replica_groups=mesh['row'=8,'col'=16] {'row','col'}, dimensions={0} | all-to-all | bytes 2359296 | tf_op jit(solution)/shard_map/all_to_all | solution.py:11
  147.2 5.7 %all-to-all-start.2 = ((f32[128,6,384]{2,1,0:T(8,128)}), f32[128,6,384]{2,1,0:T(8,128)S(1)}, u32[]{:S(2)}, u32[]{:S(2)}) async-start(f32[128,6,384]{2,1,0:T(8,128)} %broadcast_in_dim.6), calls=%async_computation.2 | async-start | bytes 3145728 | tf_op jit(solution)/shard_map/all_to_all | solution.py:19
  153.5 5.9 %convolution_bitcast_fusion = f32[384,1848]{0,1:T(8,128)} fusion(bf16[1024,1848]{1,0:T(8,128)(2,1)} %copy-done.2, bf16[384,1024]{1,0:T(8,128)(2,1)S(1)} %copy-done.10), kind=kOutput, calls=%fused_computation.3 | convolution fusion | flops 1453326336 | bytes 7409664 | tf_op jit(solution)/shard_map/dot_general | solution.py:73
  159.4 22.1 %all-to-all-done.2 = f32[128,6,384]{2,1,0:T(8,128)S(1)} async-done(((f32[128,6,384]{2,1,0:T(8,128)}), f32[128,6,384]{2,1,0:T(8,128)S(1)}, u32[]{:S(2)}, u32[]{:S(2)}) %all-to-all-start.2) | async-done | bytes 1179680 | tf_op jit(solution)/shard_map/all_to_all | solution.py:19
  184.1 11.7 %custom-call.10 = f32[128,128]{1,0:T(8,128)S(1)} custom-call(f32[128,128]{1,0:T(8,128)S(1)} %slice.40), custom_call_target="Cholesky" | custom-call | tf_op jit(solution)/shard_map/cholesky/custom-call.1 | solution.py:37
  197.2 9.8 %custom-call.11 = f32[1,128,128]{1,2,0:T(8,128)S(1)} custom-call(f32[1,128,128]{2,1,0:T(8,128)S(1)} %fusion.8), custom_call_target="InvertDiagBlocksLowerTriangular" | custom-call | tf_op jit(solution)/shard_map/triangular_solve/custom-call.0 | solution.py:38
  213.1 11.7 %custom-call.12 = f32[128,128]{1,0:T(8,128)S(1)} custom-call(f32[128,128]{1,0:T(8,128)S(1)} %convolution_subtract_fusion.3), custom_call_target="Cholesky" | custom-call | tf_op jit(solution)/shard_map/cholesky/custom-call.1 | solution.py:37
  226.0 9.8 %custom-call.13 = f32[1,128,128]{1,2,0:T(8,128)S(1)} custom-call(f32[1,128,128]{2,1,0:T(8,128)S(1)} %fusion.9), custom_call_target="InvertDiagBlocksLowerTriangular" | custom-call | tf_op jit(solution)/shard_map/triangular_solve/custom-call.0 | solution.py:38
  236.7 11.7 %custom-call.14 = f32[128,128]{1,0:T(8,128)S(1)} custom-call(f32[128,128]{1,0:T(8,128)S(1)} %convolution_subtract_fusion), custom_call_target="Cholesky" | custom-call | tf_op jit(solution)/shard_map/cholesky/custom-call.1 | solution.py:37
  249.6 10.0 %custom-call.15 = f32[1,128,128]{1,2,0:T(8,128)S(1)} custom-call(f32[1,128,128]{2,1,0:T(8,128)S(1)} %fusion.10), custom_call_target="InvertDiagBlocksLowerTriangular" | custom-call | tf_op jit(solution)/shard_map/triangular_solve/custom-call.0 | solution.py:38
  260.4 5.6 %all-to-all-start.6 = ((f32[8,96,48]{1,2,0:T(8,128)}), f32[8,96,48]{1,2,0:T(8,128)S(1)}, u32[]{:S(2)}, u32[]{:S(2)}) async-start(f32[8,96,48]{1,2,0:T(8,128)} %broadcast_in_dim.8), calls=%async_computation.7 | async-start | bytes 393216 | tf_op jit(solution)/shard_map/all_to_all | solution.py:19
  266.3 6.6 %all-to-all-done.6 = f32[8,96,48]{1,2,0:T(8,128)S(1)} async-done(((f32[8,96,48]{1,2,0:T(8,128)}), f32[8,96,48]{1,2,0:T(8,128)S(1)}, u32[]{:S(2)}, u32[]{:S(2)}) %all-to-all-start.6) | async-done | bytes 147488 | tf_op jit(solution)/shard_map/all_to_all | solution.py:19
  280.1 20.4 %all-to-all-done.3 = f32[16,64,384]{2,1,0:T(8,128)S(1)} async-done(((f32[16,64,384]{2,1,0:T(8,128)}), f32[16,64,384]{2,1,0:T(8,128)S(1)}, u32[]{:S(2)}, u32[]{:S(2)}) %all-to-all-start.3) | async-done | bytes 1572896 | tf_op jit(solution)/shard_map/all_to_all | solution.py:11
  301.9 4.4 %all-to-all-start.4 = ((f32[16,64,384]{2,1,0:T(8,128)}), f32[16,64,384]{2,1,0:T(8,128)}, u32[]{:S(2)}, u32[]{:S(2)}) async-start(f32[16,64,384]{2,1,0:T(8,128)} %broadcast_in_dim.7), calls=%async_computation.5 | async-start | bytes 3145728 | tf_op jit(solution)/shard_map/all_to_all | solution.py:19
  308.0 21.9 %all-to-all-done.4 = f32[16,64,384]{2,1,0:T(8,128)} async-done(((f32[16,64,384]{2,1,0:T(8,128)}), f32[16,64,384]{2,1,0:T(8,128)}, u32[]{:S(2)}, u32[]{:S(2)}) %all-to-all-start.4) | async-done | bytes 1572896 | tf_op jit(solution)/shard_map/all_to_all | solution.py:19
  (84 shorter events, 37.1 us)
Async XLA Ops:
  8.0 77.5 %copy-start = (bf16[768,1848]{0,1:T(8,128)(2,1)S(1)}, bf16[768,1848]{0,1:T(8,128)(2,1)}, u32[]{:S(2)}) copy-start(bf16[768,1848]{0,1:T(8,128)(2,1)} %param.14) | copy-start | bytes 8515588
  21.5 56.2 %all-to-all-start = ((bf16[16,64,1848]{2,1,0:T(8,128)(2,1)}), bf16[16,64,1848]{2,1,0:T(8,128)(2,1)}, u32[]{:S(2)}, u32[]{:S(2)}) async-start(bf16[16,64,1848]{2,1,0:T(8,128)(2,1)} %bitcast.84), calls=%async_computation | async-start | bytes 7864320 | tf_op jit(solution)/shard_map/all_to_all | solution.py:65
  28.7 153.0 %reduce-scatter.2.cloned.1.call-start = ((), (), s32[]{:S(2)}) async-start(), calls=%async_computation.8 | async-start | bytes 2506752 | tf_op jit(solution)/shard_map/reduce_scatter | solution.py:72
  77.7 4.4 %copy-start.6 = (bf16[768,1024]{1,0:T(8,128)(2,1)S(1)}, bf16[768,1024]{1,0:T(8,128)(2,1)}, u32[]{:S(2)}) copy-start(bf16[768,1024]{1,0:T(8,128)(2,1)} %param.13) | copy-start | bytes 4718596
  82.1 3.4 copy-start.2
  95.2 1.4 copy-start.9
  96.5 5.6 %copy-start.7 = (bf16[768,1024]{1,0:T(8,128)(2,1)S(1)}, bf16[768,1024]{1,0:T(8,128)(2,1)}, u32[]{:S(2)}) copy-start(bf16[768,1024]{1,0:T(8,128)(2,1)} %param.13) | copy-start | bytes 4718596
  146.0 7.5 %copy-start.10 = (bf16[384,1024]{1,0:T(8,128)(2,1)S(1)}, bf16[384,1024]{1,0:T(8,128)(2,1)}, u32[]{:S(2)}) copy-start(bf16[384,1024]{1,0:T(8,128)(2,1)} %param.12) | copy-start | bytes 2359300
  147.2 34.3 %all-to-all-start.2 = ((f32[128,6,384]{2,1,0:T(8,128)}), f32[128,6,384]{2,1,0:T(8,128)S(1)}, u32[]{:S(2)}, u32[]{:S(2)}) async-start(f32[128,6,384]{2,1,0:T(8,128)} %broadcast_in_dim.6), calls=%async_computation.2 | async-start | bytes 3145728 | tf_op jit(solution)/shard_map/all_to_all | solution.py:19
  153.0 177.0 %all-reduce.2.cloned.1.call-start = ((), (), s32[]{:S(2)}) async-start(), calls=%async_computation.9 | async-start | bytes 5677056 | tf_op jit(solution)/shard_map/psum | solution.py:74
  183.8 24.9 %copy-start.8 = (f32[768,48]{0,1:T(8,128)S(1)}, f32[768,48]{0,1:T(8,128)}, u32[]{:S(2)}) copy-start(f32[768,48]{0,1:T(8,128)} %reduce-scatter.2.cloned.1.call-done) | copy-start | bytes 442372
  207.3 65.6 %copy-start.4 = (f32[128,128]{1,0:T(8,128)}, f32[128,128]{1,0:T(8,128)S(1)}, u32[]{:S(2)}) copy-start(f32[128,128]{1,0:T(8,128)S(1)} %fusion.6) | copy-start | bytes 196612
  209.5 50.2 %all-to-all-start.5 = ((f32[8,96,48]{1,2,0:T(8,128)}), f32[8,96,48]{1,2,0:T(8,128)S(1)}, u32[]{:S(2)}, u32[]{:S(2)}) async-start(f32[8,96,48]{1,2,0:T(8,128)} %copy.25), calls=%async_computation.6 | async-start | bytes 393216 | tf_op jit(solution)/shard_map/all_to_all | solution.py:11
  260.4 12.5 %all-to-all-start.6 = ((f32[8,96,48]{1,2,0:T(8,128)}), f32[8,96,48]{1,2,0:T(8,128)S(1)}, u32[]{:S(2)}, u32[]{:S(2)}) async-start(f32[8,96,48]{1,2,0:T(8,128)} %broadcast_in_dim.8), calls=%async_computation.7 | async-start | bytes 393216 | tf_op jit(solution)/shard_map/all_to_all | solution.py:19
  272.9 27.6 %all-to-all-start.3 = ((f32[16,64,384]{2,1,0:T(8,128)}), f32[16,64,384]{2,1,0:T(8,128)S(1)}, u32[]{:S(2)}, u32[]{:S(2)}) async-start(f32[16,64,384]{2,1,0:T(8,128)} %bitcast.3), calls=%async_computation.4 | async-start | bytes 3145728 | tf_op jit(solution)/shard_map/all_to_all | solution.py:11
  300.6 6.6 %copy-start.5 = (f32[128,128]{1,0:T(8,128)S(1)}, f32[128,128]{1,0:T(8,128)}, u32[]{:S(2)}) copy-start(f32[128,128]{1,0:T(8,128)} %copy-done.4) | copy-start | bytes 196612
  301.9 28.1 %all-to-all-start.4 = ((f32[16,64,384]{2,1,0:T(8,128)}), f32[16,64,384]{2,1,0:T(8,128)}, u32[]{:S(2)}, u32[]{:S(2)}) async-start(f32[16,64,384]{2,1,0:T(8,128)} %broadcast_in_dim.7), calls=%async_computation.5 | async-start | bytes 3145728 | tf_op jit(solution)/shard_map/all_to_all | solution.py:19
  330.0 2.8 copy-start.3
  330.0 4.4 %copy-start.1 = (bf16[768,1848]{0,1:T(8,128)(2,1)S(1)}, bf16[768,1848]{0,1:T(8,128)(2,1)}, u32[]{:S(2)}) copy-start(bf16[768,1848]{0,1:T(8,128)(2,1)} %param.14) | copy-start | bytes 8515588
Sparse Core Ops, SparseCore 0:
  95.3 80.6 reduce-scatter.1
Sparse Core Ops, SparseCore 1:
  159.5 92.1 all-reduce.1
where the time goes:
time: 346 us; the launch traced here: 342 us
  waiting for transfers between devices  114 us (33%)
  other arithmetic  73.9 us (21%)
  matrix products  38.7 us (11%)
  blocking collectives  36.7 us (11%)
  local copies, waits for them, and re-layouts  31.9 us (9%)
  starting transfers between devices  30.9 us (9%)
  between operations  16.1 us (5%)
    all_to_all x3, waiting for transfers between devices, gather_rows(): return lax.all_to_all(tiled, axis, split_axis=0, concat_axis=0, tiled=True)  50.7 us
    all_to_all x1, waiting for transfers between devices, local(): lax.all_to_all(by_target, 'col', split_axis=0, concat_axis=0, tiled=True)  42.6 us
    another operation x9, other arithmetic, cholesky_solve(): low[j, j] = lax.linalg.cholesky(a, symmetrize_input=False)  37.2 us
    all_to_all x1, blocking collectives, scatter_sum(): got = lax.all_to_all(part, axis, split_axis=0, concat_axis=0, tiled=True)  36.7 us
    another operation x6, other arithmetic, cholesky_solve(): lax.linalg.triangular_solve(low[j, j], eye, left_side=True, lower=True)  31.4 us
    all_to_all x2, waiting for transfers between devices, scatter_sum(): got = lax.all_to_all(part, axis, split_axis=0, concat_axis=0, tiled=True)  20.4 us
    all_to_all x3, starting transfers between devices, gather_rows(): return lax.all_to_all(tiled, axis, split_axis=0, concat_axis=0, tiled=True)  15.7 us
    reshape x2, local copies, waits for them, and re-layouts, local(): by_target = adjusted_rows.reshape(height, ncol, width).transpose(1, 0, 2)  13.5 us
  transfers between devices with their start and end apart: 8, of which 5 were waited for; matrix products, arithmetic and copies ran while one was open for 31% of the time, Pallas kernels for 0%

commit v1 on v0

--- a/solution.py
+++ b/solution.py
@@ -80,8 +80,9 @@
     projected, range_part, own_columns = lax.optimization_barrier(
         (projected, range_part, own_columns)
     )
+    range_sketch = gather_rows(scatter_sum(range_part, "col", ncol), "col", ncol)
+    range_sketch, own_columns = lax.optimization_barrier((range_sketch, own_columns))
     own_columns = gather_rows(scatter_sum(own_columns, "row", nrow), "row", nrow)
-    range_sketch = gather_rows(scatter_sum(range_part, "col", ncol), "col", ncol)
     gram_matrix = jnp.dot(projected.T, projected, precision=highest)
     right_hand = jnp.dot(projected.T, own_columns, precision=highest)
     core_solution = cholesky_solve(gram_matrix, right_hand)

time: 346 us -> 323 us (0.934)
  waiting for transfers between devices: 114 us -> 79.4 us
  local copies, waits for them, and re-layouts: 31.9 us -> 35.5 us
    all_to_all x2, waiting for transfers between devices: 20.4 us -> 0.01 us  [scatter_sum(): got = lax.all_to_all(part, axis, split_axis=0, concat_axis=0, tiled=True)]
    all_to_all x3, waiting for transfers between devices: 50.7 us -> 36.8 us  [gather_rows(): return lax.all_to_all(tiled, axis, split_axis=0, concat_axis=0, tiled=True)]
    unnamed x25 -> x35, local copies, waits for them, and re-layouts: 12.1 us -> 13.1 us
  transfers between devices with their start and end apart: 8 -> 8, of which waited for: 5 -> 4; matrix products, arithmetic and copies ran while one was open for 31% -> 35% of each run, Pallas kernels for 0% -> 0%
where the time goes in v1:
time: 323 us; the launch traced here: 319 us
  waiting for transfers between devices  79.4 us (25%)
  other arithmetic  76.6 us (24%)
  matrix products  40.9 us (13%)
  blocking collectives  36.7 us (11%)
  local copies, waits for them, and re-layouts  35.5 us (11%)
  starting transfers between devices  33.8 us (10%)
  between operations  16.2 us (5%)
    all_to_all x1, waiting for transfers between devices, local(): lax.all_to_all(by_target, 'col', split_axis=0, concat_axis=0, tiled=True)  42.6 us
    another operation x9, other arithmetic, cholesky_solve(): low[j, j] = lax.linalg.cholesky(a, symmetrize_input=False)  38 us
    all_to_all x3, waiting for transfers between devices, gather_rows(): return lax.all_to_all(tiled, axis, split_axis=0, concat_axis=0, tiled=True)  36.8 us
    all_to_all x1, blocking collectives, scatter_sum(): got = lax.all_to_all(part, axis, split_axis=0, concat_axis=0, tiled=True)  36.7 us
    another operation x6, other arithmetic, cholesky_solve(): lax.linalg.triangular_solve(low[j, j], eye, left_side=True, lower=True)  32.7 us
    all_to_all x3, starting transfers between devices, gather_rows(): return lax.all_to_all(tiled, axis, split_axis=0, concat_axis=0, tiled=True)  18.8 us
    reshape x2, local copies, waits for them, and re-layouts, local(): by_target = adjusted_rows.reshape(height, ncol, width).transpose(1, 0, 2)  13.4 us
    unnamed x35, local copies, waits for them, and re-layouts  13.1 us
  transfers between devices with their start and end apart: 8, of which 4 were waited for; matrix products, arithmetic and copies ran while one was open for 35% of the time, Pallas kernels for 0%

profile of v1, /device:TPU:0, one launch (start us, length us, event | category | flops | bytes accessed | tf_op | source)
XLA Modules:
  0.0 319.1 jit_solution(2407146626221024432)
XLA Ops:
  8.0 8.6 %reshape.49 = bf16[64,16,1848]{2,1,0:T(8,128)(2,1)} reshape(bf16[64,29568]{1,0:T(8,128)(2,1)} %param.9) | data formatting | bytes 7569408 | tf_op jit(solution)/shard_map/reshape | solution.py:64
  16.6 4.9 %copy.30 = bf16[64,16,1848]{2,0,1:T(8,128)(2,1)} copy(bf16[64,16,1848]{2,1,0:T(8,128)(2,1)} %reshape.49) | data formatting | bytes 7569408 | tf_op jit(solution)/shard_map/reshape | solution.py:64
  21.5 7.2 %all-to-all-start = ((bf16[16,64,1848]{2,1,0:T(8,128)(2,1)}), bf16[16,64,1848]{2,1,0:T(8,128)(2,1)}, u32[]{:S(2)}, u32[]{:S(2)}) async-start(bf16[16,64,1848]{2,1,0:T(8,128)(2,1)} %bitcast.84), calls=%async_computation | async-start | bytes 7864320 | tf_op jit(solution)/shard_map/all_to_all | solution.py:65
  28.7 6.4 %copy.22 = bf16[1024,1848]{1,0:T(8,128)(2,1)} copy(bf16[1024,1848]{0,1:T(8,128)(2,1)} %param.10) | data formatting | bytes 7569408 | tf_op args[1]
  35.1 42.6 %all-to-all-done = bf16[16,64,1848]{2,1,0:T(8,128)(2,1)} async-done(((bf16[16,64,1848]{2,1,0:T(8,128)(2,1)}), bf16[16,64,1848]{2,1,0:T(8,128)(2,1)}, u32[]{:S(2)}, u32[]{:S(2)}) %all-to-all-start) | async-done | bytes 3784736 | tf_op jit(solution)/shard_map/all_to_all | solution.py:65
  77.7 4.4 %fusion = bf16[1024,1848]{1,0:T(8,128)(2,1)S(1)} fusion(bf16[1024,1848]{1,0:T(8,128)(2,1)} %copy.22, bf16[16,64,1848]{2,1,0:T(8,128)(2,1)} %all-to-all-done), kind=kLoop, calls=%fused_computation.1 | loop fusion | flops 7569408 | bytes 11354112 | tf_op jit(solution)/shard_map/convert_element_type | solution.py:67
  85.5 9.7 %fusion.22 = f32[768,768]{0,1:T(8,128)} fusion(f32[1848,768]{1,0:T(8,128)S(1)} %fusion.21, bf16[768,1848]{0,1:T(8,128)(2,1)S(1)} %copy-done), kind=kOutput, calls=%fused_computation.49 | convolution fusion | flops 13079937024 | bytes 10874880 | tf_op jit(solution)/shard_map/dot_general | solution.py:71
  96.5 5.6 %fusion.20 = f32[1024,384]{1,0:T(8,128)} fusion(bf16[1024,1848]{1,0:T(8,128)(2,1)} %copy-done.3, bf16[1848,384]{1,0:T(8,128)(2,1)S(1)} %copy-done.14), kind=kOutput, calls=%fused_computation.47 | convolution fusion | flops 1453326336 | bytes 6776832 | tf_op jit(solution)/shard_map/dot_general | solution.py:75
  102.1 5.3 %convolution_bitcast_fusion.1 = f32[768,384]{0,1:T(8,128)S(1)} fusion(f32[1024,384]{1,0:T(8,128)} %fusion.20, bf16[768,1024]{1,0:T(8,128)(2,1)S(1)} %copy-done.10), kind=kOutput, calls=%fused_computation.4 | convolution fusion | flops 3623878656 | bytes 4325376 | tf_op jit(solution)/shard_map/dot_general | solution.py:77
  109.1 36.7 %all_to_all.59 = f32[128,6,384]{2,1,0:T(8,128)S(1)} all-to-all(f32[128,6,384]{2,1,0:T(8,128)} %all_to_all.40), channel_id=1, replica_groups=mesh['row'=8,'col'=16] {'row','col'}, dimensions={0} | all-to-all | bytes 2359296 | tf_op jit(solution)/shard_map/all_to_all | solution.py:11
  147.2 5.7 %all-to-all-start.2 = ((f32[128,6,384]{2,1,0:T(8,128)}), f32[128,6,384]{2,1,0:T(8,128)S(1)}, u32[]{:S(2)}, u32[]{:S(2)}) async-start(f32[128,6,384]{2,1,0:T(8,128)} %broadcast_in_dim.6), calls=%async_computation.2 | async-start | bytes 3145728 | tf_op jit(solution)/shard_map/all_to_all | solution.py:19
  153.5 5.9 %convolution_bitcast_fusion = f32[384,1848]{0,1:T(8,128)} fusion(bf16[1024,1848]{1,0:T(8,128)(2,1)} %copy-done.3, bf16[384,1024]{1,0:T(8,128)(2,1)S(1)} %copy-done.15), kind=kOutput, calls=%fused_computation.3 | convolution fusion | flops 1453326336 | bytes 7409664 | tf_op jit(solution)/shard_map/dot_general | solution.py:73
  159.4 22.1 %all-to-all-done.2 = f32[128,6,384]{2,1,0:T(8,128)S(1)} async-done(((f32[128,6,384]{2,1,0:T(8,128)}), f32[128,6,384]{2,1,0:T(8,128)S(1)}, u32[]{:S(2)}, u32[]{:S(2)}) %all-to-all-start.2) | async-done | bytes 1179680 | tf_op jit(solution)/shard_map/all_to_all | solution.py:19
  184.1 11.7 %custom-call.10 = f32[128,128]{1,0:T(8,128)S(1)} custom-call(f32[128,128]{1,0:T(8,128)S(1)} %slice.40), custom_call_target="Cholesky" | custom-call | tf_op jit(solution)/shard_map/cholesky/custom-call.1 | solution.py:37
  195.8 3.9 %all-to-all-start.3 = ((f32[16,64,384]{2,1,0:T(8,128)}), f32[16,64,384]{2,1,0:T(8,128)S(1)}, u32[]{:S(2)}, u32[]{:S(2)}) async-start(f32[16,64,384]{2,1,0:T(8,128)} %bitcast.3), calls=%async_computation.4 | async-start | bytes 3145728 | tf_op jit(solution)/shard_map/all_to_all | solution.py:11
  201.0 9.8 %custom-call.11 = f32[1,128,128]{1,2,0:T(8,128)S(1)} custom-call(f32[1,128,128]{2,1,0:T(8,128)S(1)} %fusion.8), custom_call_target="InvertDiagBlocksLowerTriangular" | custom-call | tf_op jit(solution)/shard_map/triangular_solve/custom-call.0 | solution.py:38
  212.9 12.5 %custom-call.12 = f32[128,128]{1,0:T(8,128)S(1)} custom-call(f32[128,128]{1,0:T(8,128)} %convolution_subtract_fusion.3), custom_call_target="Cholesky" | custom-call | tf_op jit(solution)/shard_map/cholesky/custom-call.1 | solution.py:37
  227.3 10.6 %custom-call.13 = f32[1,128,128]{1,2,0:T(8,128)S(1)} custom-call(f32[1,128,128]{2,1,0:T(8,128)} %fusion.9), custom_call_target="InvertDiagBlocksLowerTriangular" | custom-call | tf_op jit(solution)/shard_map/triangular_solve/custom-call.0 | solution.py:38
  240.9 7.5 %all-to-all-start.4 = ((f32[16,64,384]{2,1,0:T(8,128)}), f32[16,64,384]{2,1,0:T(8,128)S(1)}, u32[]{:S(2)}, u32[]{:S(2)}) async-start(f32[16,64,384]{2,1,0:T(8,128)} %broadcast_in_dim.7), calls=%async_computation.5 | async-start | bytes 3145728 | tf_op jit(solution)/shard_map/all_to_all | solution.py:19
  251.2 11.7 %custom-call.14 = f32[128,128]{1,0:T(8,128)S(1)} custom-call(f32[128,128]{1,0:T(8,128)S(1)} %convolution_subtract_fusion), custom_call_target="Cholesky" | custom-call | tf_op jit(solution)/shard_map/cholesky/custom-call.1 | solution.py:37
  263.6 8.7 %all-to-all-done.4 = f32[16,64,384]{2,1,0:T(8,128)S(1)} async-done(((f32[16,64,384]{2,1,0:T(8,128)}), f32[16,64,384]{2,1,0:T(8,128)S(1)}, u32[]{:S(2)}, u32[]{:S(2)}) %all-to-all-start.4) | async-done | bytes 1572896 | tf_op jit(solution)/shard_map/all_to_all | solution.py:19
  278.2 9.8 %custom-call.15 = f32[1,128,128]{1,2,0:T(8,128)S(1)} custom-call(f32[1,128,128]{2,1,0:T(8,128)S(1)} %fusion.10), custom_call_target="InvertDiagBlocksLowerTriangular" | custom-call | tf_op jit(solution)/shard_map/triangular_solve/custom-call.0 | solution.py:38
  288.8 5.6 %all-to-all-start.6 = ((f32[8,96,48]{1,2,0:T(8,128)}), f32[8,96,48]{1,2,0:T(8,128)S(1)}, u32[]{:S(2)}, u32[]{:S(2)}) async-start(f32[8,96,48]{1,2,0:T(8,128)} %broadcast_in_dim.8), calls=%async_computation.7 | async-start | bytes 393216 | tf_op jit(solution)/shard_map/all_to_all | solution.py:19
  295.3 6.0 %all-to-all-done.6 = f32[8,96,48]{1,2,0:T(8,128)S(1)} async-done(((f32[8,96,48]{1,2,0:T(8,128)}), f32[8,96,48]{1,2,0:T(8,128)S(1)}, u32[]{:S(2)}, u32[]{:S(2)}) %all-to-all-start.6) | async-done | bytes 147488 | tf_op jit(solution)/shard_map/all_to_all | solution.py:19
  (94 shorter events, 40.1 us)
Async XLA Ops:
  8.0 77.5 %copy-start = (bf16[768,1848]{0,1:T(8,128)(2,1)S(1)}, bf16[768,1848]{0,1:T(8,128)(2,1)}, u32[]{:S(2)}) copy-start(bf16[768,1848]{0,1:T(8,128)(2,1)} %param.14) | copy-start | bytes 8515588
  21.5 56.2 %all-to-all-start = ((bf16[16,64,1848]{2,1,0:T(8,128)(2,1)}), bf16[16,64,1848]{2,1,0:T(8,128)(2,1)}, u32[]{:S(2)}, u32[]{:S(2)}) async-start(bf16[16,64,1848]{2,1,0:T(8,128)(2,1)} %bitcast.84), calls=%async_computation | async-start | bytes 7864320 | tf_op jit(solution)/shard_map/all_to_all | solution.py:65
  28.7 153.0 %reduce-scatter.2.cloned.1.call-start = ((), (), s32[]{:S(2)}) async-start(), calls=%async_computation.8 | async-start | bytes 2506752 | tf_op jit(solution)/shard_map/reduce_scatter | solution.py:72
  77.7 4.4 %copy-start.9 = (bf16[768,1024]{1,0:T(8,128)(2,1)S(1)}, bf16[768,1024]{1,0:T(8,128)(2,1)}, u32[]{:S(2)}) copy-start(bf16[768,1024]{1,0:T(8,128)(2,1)} %param.13) | copy-start | bytes 4718596
  82.0 3.4 %copy-start.3 = (bf16[1024,1848]{1,0:T(8,128)(2,1)}, bf16[1024,1848]{1,0:T(8,128)(2,1)S(1)}, u32[]{:S(2)}) copy-start(bf16[1024,1848]{1,0:T(8,128)(2,1)S(1)} %fusion) | copy-start | bytes 11354116
  95.1 1.4 copy-start.14
  96.5 5.6 %copy-start.10 = (bf16[768,1024]{1,0:T(8,128)(2,1)S(1)}, bf16[768,1024]{1,0:T(8,128)(2,1)}, u32[]{:S(2)}) copy-start(bf16[768,1024]{1,0:T(8,128)(2,1)} %param.13) | copy-start | bytes 4718596
  146.0 7.5 %copy-start.15 = (bf16[384,1024]{1,0:T(8,128)(2,1)S(1)}, bf16[384,1024]{1,0:T(8,128)(2,1)}, u32[]{:S(2)}) copy-start(bf16[384,1024]{1,0:T(8,128)(2,1)} %param.12) | copy-start | bytes 2359300
  147.2 34.3 %all-to-all-start.2 = ((f32[128,6,384]{2,1,0:T(8,128)}), f32[128,6,384]{2,1,0:T(8,128)S(1)}, u32[]{:S(2)}, u32[]{:S(2)}) async-start(f32[128,6,384]{2,1,0:T(8,128)} %broadcast_in_dim.6), calls=%async_computation.2 | async-start | bytes 3145728 | tf_op jit(solution)/shard_map/all_to_all | solution.py:19
  153.0 154.1 %all-reduce.2.cloned.1.call-start = ((), (), s32[]{:S(2)}) async-start(), calls=%async_computation.9 | async-start | bytes 5677056 | tf_op jit(solution)/shard_map/psum | solution.py:74
  195.8 42.2 %all-to-all-start.3 = ((f32[16,64,384]{2,1,0:T(8,128)}), f32[16,64,384]{2,1,0:T(8,128)S(1)}, u32[]{:S(2)}, u32[]{:S(2)}) async-start(f32[16,64,384]{2,1,0:T(8,128)} %bitcast.3), calls=%async_computation.4 | async-start | bytes 3145728 | tf_op jit(solution)/shard_map/all_to_all | solution.py:11
  211.1 0.6 copy-start.5
  240.9 31.4 %all-to-all-start.4 = ((f32[16,64,384]{2,1,0:T(8,128)}), f32[16,64,384]{2,1,0:T(8,128)S(1)}, u32[]{:S(2)}, u32[]{:S(2)}) async-start(f32[16,64,384]{2,1,0:T(8,128)} %broadcast_in_dim.7), calls=%async_computation.5 | async-start | bytes 3145728 | tf_op jit(solution)/shard_map/all_to_all | solution.py:19
  248.7 2.0 copy-start.11
  250.3 0.6 copy-start.7
  251.0 52.9 %copy-start.6 = (f32[128,128]{1,0:T(8,128)S(1)}, f32[128,128]{1,0:T(8,128)}, u32[]{:S(2)}) copy-start(f32[128,128]{1,0:T(8,128)} %copy-done.5) | copy-start | bytes 196612
  251.2 53.1 %copy-start.12 = (f32[128,128]{1,0:T(8,128)S(1)}, f32[128,128]{1,0:T(8,128)}, u32[]{:S(2)}) copy-start(f32[128,128]{1,0:T(8,128)} %copy-done.11) | copy-start | bytes 196612
  272.3 32.3 %copy-start.2 = (f32[16,64,384]{2,1,0:T(8,128)}, f32[16,64,384]{2,1,0:T(8,128)S(1)}, u32[]{:S(2)}) copy-start(f32[16,64,384]{2,1,0:T(8,128)S(1)} %all-to-all-done.4) | copy-start | bytes 4718596
  272.3 32.6 %copy-start.8 = (f32[128,128]{1,0:T(8,128)S(1)}, f32[128,128]{1,0:T(8,128)}, u32[]{:S(2)}) copy-start(f32[128,128]{1,0:T(8,128)} %copy-done.7) | copy-start | bytes 196612
  274.3 13.8 %all-to-all-start.5 = ((f32[8,96,48]{1,2,0:T(8,128)}), f32[8,96,48]{1,2,0:T(8,128)S(1)}, u32[]{:S(2)}, u32[]{:S(2)}) async-start(f32[8,96,48]{1,2,0:T(8,128)} %copy.25), calls=%async_computation.6 | async-start | bytes 393216 | tf_op jit(solution)/shard_map/all_to_all | solution.py:11
  288.8 12.6 %all-to-all-start.6 = ((f32[8,96,48]{1,2,0:T(8,128)}), f32[8,96,48]{1,2,0:T(8,128)S(1)}, u32[]{:S(2)}, u32[]{:S(2)}) async-start(f32[8,96,48]{1,2,0:T(8,128)} %broadcast_in_dim.8), calls=%async_computation.7 | async-start | bytes 393216 | tf_op jit(solution)/shard_map/all_to_all | solution.py:19
  301.4 3.7 %copy-start.13 = (f32[128,128]{1,0:T(8,128)S(1)}, f32[128,128]{1,0:T(8,128)}, u32[]{:S(2)}) copy-start(f32[128,128]{1,0:T(8,128)} %fusion.2) | copy-start | bytes 196612
  307.1 2.8 copy-start.4
  307.1 4.4 %copy-start.1 = (bf16[768,1848]{0,1:T(8,128)(2,1)S(1)}, bf16[768,1848]{0,1:T(8,128)(2,1)}, u32[]{:S(2)}) copy-start(bf16[768,1848]{0,1:T(8,128)(2,1)} %param.14) | copy-start | bytes 8515588
Sparse Core Ops, SparseCore 0:
  95.3 80.6 reduce-scatter.1
Sparse Core Ops, SparseCore 1:
  159.5 94.3 all-reduce.1

commit v2 on v1

--- a/solution.py
+++ b/solution.py
@@ -75,8 +75,8 @@
     range_part = jnp.dot(difference, range_test, preferred_element_type=jnp.float32)
     left_float = core_left.astype(jnp.float32)
     projected_part = jnp.dot(left_float, range_part, precision=highest)
-    every = ("row", "col")
-    projected = gather_rows(scatter_sum(projected_part, every, nrow * ncol), every, nrow * ncol)
+    projected = scatter_sum(scatter_sum(projected_part, "col", ncol), "row", nrow)
+    projected = gather_rows(gather_rows(projected, "row", nrow), "col", ncol)
     projected, range_part, own_columns = lax.optimization_barrier(
         (projected, range_part, own_columns)
     )

time: 323 us -> 324 us (level)
  blocking collectives: 36.7 us -> 43 us
    all_to_all x0 -> x1, blocking collectives: none -> 8.94 us  [gather_rows(): return lax.all_to_all(tiled, axis, split_axis=0, concat_axis=0, tiled=True)]
    all_to_all x1 -> x2, blocking collectives: 36.7 us -> 34 us  [scatter_sum(): got = lax.all_to_all(part, axis, split_axis=0, concat_axis=0, tiled=True)]
where the time goes in v2:
time: 324 us; the launch traced here: 320 us
  waiting for transfers between devices  77.3 us (24%)
  other arithmetic  76.9 us (24%)
  blocking collectives  43 us (13%)
  matrix products  40.9 us (13%)
  local copies, waits for them, and re-layouts  33.9 us (10%)
  starting transfers between devices  31.8 us (10%)
  between operations  16.2 us (5%)
    all_to_all x1, waiting for transfers between devices, local(): lax.all_to_all(by_target, 'col', split_axis=0, concat_axis=0, tiled=True)  42.6 us
    another operation x9, other arithmetic, cholesky_solve(): low[j, j] = lax.linalg.cholesky(a, symmetrize_input=False)  38.1 us
    all_to_all x3, waiting for transfers between devices, gather_rows(): return lax.all_to_all(tiled, axis, split_axis=0, concat_axis=0, tiled=True)  34.7 us
    all_to_all x2, blocking collectives, scatter_sum(): got = lax.all_to_all(part, axis, split_axis=0, concat_axis=0, tiled=True)  34 us
    another operation x6, other arithmetic, cholesky_solve(): lax.linalg.triangular_solve(low[j, j], eye, left_side=True, lower=True)  32.9 us
    all_to_all x3, starting transfers between devices, gather_rows(): return lax.all_to_all(tiled, axis, split_axis=0, concat_axis=0, tiled=True)  16.8 us
    reshape x2, local copies, waits for them, and re-layouts, local(): by_target = adjusted_rows.reshape(height, ncol, width).transpose(1, 0, 2)  13.5 us
    unnamed x35, local copies, waits for them, and re-layouts  13.1 us
  transfers between devices with their start and end apart: 8, of which 4 were waited for; matrix products, arithmetic and copies ran while one was open for 35% of the time, Pallas kernels for 0%

profile of v2, /device:TPU:0, one launch (start us, length us, event | category | flops | bytes accessed | tf_op | source)
XLA Modules:
  0.0 320.0 jit_solution(5877116045567364182)
XLA Ops:
  8.0 8.6 %reshape.59 = bf16[64,16,1848]{2,1,0:T(8,128)(2,1)} reshape(bf16[64,29568]{1,0:T(8,128)(2,1)} %param.9) | data formatting | bytes 7569408 | tf_op jit(solution)/shard_map/reshape | solution.py:64
  16.6 4.9 %copy.30 = bf16[64,16,1848]{2,0,1:T(8,128)(2,1)} copy(bf16[64,16,1848]{2,1,0:T(8,128)(2,1)} %reshape.59) | data formatting | bytes 7569408 | tf_op jit(solution)/shard_map/reshape | solution.py:64
  21.5 7.2 %all-to-all-start = ((bf16[16,64,1848]{2,1,0:T(8,128)(2,1)}), bf16[16,64,1848]{2,1,0:T(8,128)(2,1)}, u32[]{:S(2)}, u32[]{:S(2)}) async-start(bf16[16,64,1848]{2,1,0:T(8,128)(2,1)} %bitcast.88), calls=%async_computation | async-start | bytes 7864320 | tf_op jit(solution)/shard_map/all_to_all | solution.py:65
  28.7 6.3 %copy.22 = bf16[1024,1848]{1,0:T(8,128)(2,1)} copy(bf16[1024,1848]{0,1:T(8,128)(2,1)} %param.10) | data formatting | bytes 7569408 | tf_op args[1]
  35.1 42.6 %all-to-all-done = bf16[16,64,1848]{2,1,0:T(8,128)(2,1)} async-done(((bf16[16,64,1848]{2,1,0:T(8,128)(2,1)}), bf16[16,64,1848]{2,1,0:T(8,128)(2,1)}, u32[]{:S(2)}, u32[]{:S(2)}) %all-to-all-start) | async-done | bytes 3784736 | tf_op jit(solution)/shard_map/all_to_all | solution.py:65
  77.7 4.4 %fusion = bf16[1024,1848]{1,0:T(8,128)(2,1)S(1)} fusion(bf16[1024,1848]{1,0:T(8,128)(2,1)} %copy.22, bf16[16,64,1848]{2,1,0:T(8,128)(2,1)} %all-to-all-done), kind=kLoop, calls=%fused_computation.1 | loop fusion | flops 7569408 | bytes 11354112 | tf_op jit(solution)/shard_map/convert_element_type | solution.py:67
  85.5 9.7 %fusion.22 = f32[768,768]{0,1:T(8,128)} fusion(f32[1848,768]{1,0:T(8,128)S(1)} %fusion.21, bf16[768,1848]{0,1:T(8,128)(2,1)S(1)} %copy-done), kind=kOutput, calls=%fused_computation.49 | convolution fusion | flops 13079937024 | bytes 10874880 | tf_op jit(solution)/shard_map/dot_general | solution.py:71
  96.5 5.6 %fusion.20 = f32[1024,384]{1,0:T(8,128)} fusion(bf16[1024,1848]{1,0:T(8,128)(2,1)} %copy-done.3, bf16[1848,384]{1,0:T(8,128)(2,1)S(1)} %copy-done.14), kind=kOutput, calls=%fused_computation.47 | convolution fusion | flops 1453326336 | bytes 6776832 | tf_op jit(solution)/shard_map/dot_general | solution.py:75
  102.1 5.3 %convolution_bitcast_fusion.1 = f32[768,384]{0,1:T(8,128)S(1)} fusion(f32[1024,384]{1,0:T(8,128)} %fusion.20, bf16[768,1024]{1,0:T(8,128)(2,1)S(1)} %copy-done.10), kind=kOutput, calls=%fused_computation.4 | convolution fusion | flops 3623878656 | bytes 4325376 | tf_op jit(solution)/shard_map/dot_general | solution.py:77
  107.8 22.3 %all_to_all.74 = f32[16,48,384]{2,1,0:T(8,128)S(1)} all-to-all(f32[16,48,384]{2,1,0:T(8,128)S(1)} %bitcast.90), channel_id=1, replica_groups=mesh['row'=8,'col'=16] {'col'}, dimensions={0} | all-to-all | bytes 2359296 | tf_op jit(solution)/shard_map/all_to_all | solution.py:11
  130.3 11.7 %all_to_all.75 = f32[8,6,384]{2,1,0:T(8,128)S(1)} all-to-all(f32[8,6,384]{2,1,0:T(8,128)S(1)} %all_to_all.52), channel_id=1, replica_groups=mesh['row'=8,'col'=16] {'row'}, dimensions={0} | all-to-all | bytes 147456 | tf_op jit(solution)/shard_map/all_to_all | solution.py:11
  142.0 8.9 %all_to_all.76 = f32[8,6,384]{2,1,0:T(8,128)S(1)} all-to-all(f32[8,6,384]{2,1,0:T(8,128)S(1)} %broadcast_in_dim.10), channel_id=1, replica_groups=mesh['row'=8,'col'=16] {'row'}, dimensions={0} | all-to-all | bytes 147456 | tf_op jit(solution)/shard_map/all_to_all | solution.py:19
  156.3 5.9 %convolution_bitcast_fusion = f32[384,1848]{0,1:T(8,128)} fusion(bf16[1024,1848]{1,0:T(8,128)(2,1)} %copy-done.3, bf16[384,1024]{1,0:T(8,128)(2,1)S(1)} %copy-done.15), kind=kOutput, calls=%fused_computation.3 | convolution fusion | flops 1453326336 | bytes 7409664 | tf_op jit(solution)/shard_map/dot_general | solution.py:73
  162.3 12.9 %all-to-all-done.4 = f32[16,48,384]{2,1,0:T(8,128)S(1)} async-done(((f32[16,48,384]{2,1,0:T(8,128)}), f32[16,48,384]{2,1,0:T(8,128)S(1)}, u32[]{:S(2)}, u32[]{:S(2)}) %all-to-all-start.4) | async-done | bytes 1179680 | tf_op jit(solution)/shard_map/all_to_all | solution.py:19
  177.5 11.7 %custom-call.10 = f32[128,128]{1,0:T(8,128)S(1)} custom-call(f32[128,128]{1,0:T(8,128)S(1)} %slice.40), custom_call_target="Cholesky" | custom-call | tf_op jit(solution)/shard_map/cholesky/custom-call.1 | solution.py:37
  194.5 9.8 %custom-call.11 = f32[1,128,128]{1,2,0:T(8,128)S(1)} custom-call(f32[1,128,128]{2,1,0:T(8,128)S(1)} %fusion.8), custom_call_target="InvertDiagBlocksLowerTriangular" | custom-call | tf_op jit(solution)/shard_map/triangular_solve/custom-call.0 | solution.py:38
  206.4 12.5 %custom-call.12 = f32[128,128]{1,0:T(8,128)S(1)} custom-call(f32[128,128]{1,0:T(8,128)} %convolution_subtract_fusion.3), custom_call_target="Cholesky" | custom-call | tf_op jit(solution)/shard_map/cholesky/custom-call.1 | solution.py:37
  220.9 10.6 %custom-call.13 = f32[1,128,128]{1,2,0:T(8,128)S(1)} custom-call(f32[1,128,128]{2,1,0:T(8,128)} %fusion.9), custom_call_target="InvertDiagBlocksLowerTriangular" | custom-call | tf_op jit(solution)/shard_map/triangular_solve/custom-call.0 | solution.py:38
  234.5 7.5 %all-to-all-start.6 = ((f32[16,64,384]{2,1,0:T(8,128)}), f32[16,64,384]{2,1,0:T(8,128)S(1)}, u32[]{:S(2)}, u32[]{:S(2)}) async-start(f32[16,64,384]{2,1,0:T(8,128)} %broadcast_in_dim.13), calls=%async_computation.7 | async-start | bytes 3145728 | tf_op jit(solution)/shard_map/all_to_all | solution.py:19
  244.8 11.7 %custom-call.14 = f32[128,128]{1,0:T(8,128)S(1)} custom-call(f32[128,128]{1,0:T(8,128)S(1)} %convolution_subtract_fusion), custom_call_target="Cholesky" | custom-call | tf_op jit(solution)/shard_map/cholesky/custom-call.1 | solution.py:37
  257.2 15.8 %all-to-all-done.6 = f32[16,64,384]{2,1,0:T(8,128)S(1)} async-done(((f32[16,64,384]{2,1,0:T(8,128)}), f32[16,64,384]{2,1,0:T(8,128)S(1)}, u32[]{:S(2)}, u32[]{:S(2)}) %all-to-all-start.6) | async-done | bytes 1572896 | tf_op jit(solution)/shard_map/all_to_all | solution.py:19
  279.1 9.8 %custom-call.15 = f32[1,128,128]{1,2,0:T(8,128)S(1)} custom-call(f32[1,128,128]{2,1,0:T(8,128)S(1)} %fusion.10), custom_call_target="InvertDiagBlocksLowerTriangular" | custom-call | tf_op jit(solution)/shard_map/triangular_solve/custom-call.0 | solution.py:38
  289.6 5.6 %all-to-all-start.8 = ((f32[8,96,48]{1,2,0:T(8,128)}), f32[8,96,48]{1,2,0:T(8,128)S(1)}, u32[]{:S(2)}, u32[]{:S(2)}) async-start(f32[8,96,48]{1,2,0:T(8,128)} %broadcast_in_dim.14), calls=%async_computation.9 | async-start | bytes 393216 | tf_op jit(solution)/shard_map/all_to_all | solution.py:19
  296.2 6.0 %all-to-all-done.8 = f32[8,96,48]{1,2,0:T(8,128)S(1)} async-done(((f32[8,96,48]{1,2,0:T(8,128)}), f32[8,96,48]{1,2,0:T(8,128)S(1)}, u32[]{:S(2)}, u32[]{:S(2)}) %all-to-all-start.8) | async-done | bytes 147488 | tf_op jit(solution)/shard_map/all_to_all | solution.py:19
  (98 shorter events, 46.3 us)
Async XLA Ops:
  8.0 77.5 %copy-start = (bf16[768,1848]{0,1:T(8,128)(2,1)S(1)}, bf16[768,1848]{0,1:T(8,128)(2,1)}, u32[]{:S(2)}) copy-start(bf16[768,1848]{0,1:T(8,128)(2,1)} %param.14) | copy-start | bytes 8515588
  21.5 56.2 %all-to-all-start = ((bf16[16,64,1848]{2,1,0:T(8,128)(2,1)}), bf16[16,64,1848]{2,1,0:T(8,128)(2,1)}, u32[]{:S(2)}, u32[]{:S(2)}) async-start(bf16[16,64,1848]{2,1,0:T(8,128)(2,1)} %bitcast.88), calls=%async_computation | async-start | bytes 7864320 | tf_op jit(solution)/shard_map/all_to_all | solution.py:65
  28.7 146.5 %reduce-scatter.2.cloned.1.call-start = ((), (), s32[]{:S(2)}) async-start(), calls=%async_computation.10 | async-start | bytes 2506752 | tf_op jit(solution)/shard_map/reduce_scatter | solution.py:72
  77.7 4.4 %copy-start.9 = (bf16[768,1024]{1,0:T(8,128)(2,1)S(1)}, bf16[768,1024]{1,0:T(8,128)(2,1)}, u32[]{:S(2)}) copy-start(bf16[768,1024]{1,0:T(8,128)(2,1)} %param.13) | copy-start | bytes 4718596
  82.1 3.4 %copy-start.3 = (bf16[1024,1848]{1,0:T(8,128)(2,1)}, bf16[1024,1848]{1,0:T(8,128)(2,1)S(1)}, u32[]{:S(2)}) copy-start(bf16[1024,1848]{1,0:T(8,128)(2,1)S(1)} %fusion) | copy-start | bytes 11354116
  95.2 1.4 copy-start.14
  96.5 5.6 %copy-start.10 = (bf16[768,1024]{1,0:T(8,128)(2,1)S(1)}, bf16[768,1024]{1,0:T(8,128)(2,1)}, u32[]{:S(2)}) copy-start(bf16[768,1024]{1,0:T(8,128)(2,1)} %param.13) | copy-start | bytes 4718596
  130.2 26.1 %copy-start.15 = (bf16[384,1024]{1,0:T(8,128)(2,1)S(1)}, bf16[384,1024]{1,0:T(8,128)(2,1)}, u32[]{:S(2)}) copy-start(bf16[384,1024]{1,0:T(8,128)(2,1)} %param.12) | copy-start | bytes 2359300
  152.1 23.1 %all-to-all-start.4 = ((f32[16,48,384]{2,1,0:T(8,128)}), f32[16,48,384]{2,1,0:T(8,128)S(1)}, u32[]{:S(2)}, u32[]{:S(2)}) async-start(f32[16,48,384]{2,1,0:T(8,128)} %broadcast_in_dim.12), calls=%async_computation.4 | async-start | bytes 2359296 | tf_op jit(solution)/shard_map/all_to_all | solution.py:19
  155.8 152.2 %all-reduce.2.cloned.1.call-start = ((), (), s32[]{:S(2)}) async-start(), calls=%async_computation.11 | async-start | bytes 5677056 | tf_op jit(solution)/shard_map/psum | solution.py:74
  189.3 42.3 %all-to-all-start.5 = ((f32[16,64,384]{2,1,0:T(8,128)}), f32[16,64,384]{2,1,0:T(8,128)S(1)}, u32[]{:S(2)}, u32[]{:S(2)}) async-start(f32[16,64,384]{2,1,0:T(8,128)} %bitcast.5), calls=%async_computation.6 | async-start | bytes 3145728 | tf_op jit(solution)/shard_map/all_to_all | solution.py:11
  204.6 0.6 copy-start.5
  234.5 38.6 %all-to-all-start.6 = ((f32[16,64,384]{2,1,0:T(8,128)}), f32[16,64,384]{2,1,0:T(8,128)S(1)}, u32[]{:S(2)}, u32[]{:S(2)}) async-start(f32[16,64,384]{2,1,0:T(8,128)} %broadcast_in_dim.13), calls=%async_computation.7 | async-start | bytes 3145728 | tf_op jit(solution)/shard_map/all_to_all | solution.py:19
  242.2 2.0 copy-start.11
  243.9 0.6 copy-start.7
  244.5 60.2 %copy-start.6 = (f32[128,128]{1,0:T(8,128)S(1)}, f32[128,128]{1,0:T(8,128)}, u32[]{:S(2)}) copy-start(f32[128,128]{1,0:T(8,128)} %copy-done.5) | copy-start | bytes 196612
  244.8 60.4 %copy-start.12 = (f32[128,128]{1,0:T(8,128)S(1)}, f32[128,128]{1,0:T(8,128)}, u32[]{:S(2)}) copy-start(f32[128,128]{1,0:T(8,128)} %copy-done.11) | copy-start | bytes 196612
  273.0 32.4 %copy-start.2 = (f32[16,64,384]{2,1,0:T(8,128)}, f32[16,64,384]{2,1,0:T(8,128)S(1)}, u32[]{:S(2)}) copy-start(f32[16,64,384]{2,1,0:T(8,128)S(1)} %all-to-all-done.6) | copy-start | bytes 4718596
  273.0 32.7 %copy-start.8 = (f32[128,128]{1,0:T(8,128)S(1)}, f32[128,128]{1,0:T(8,128)}, u32[]{:S(2)}) copy-start(f32[128,128]{1,0:T(8,128)} %copy-done.7) | copy-start | bytes 196612
  275.0 13.9 %all-to-all-start.7 = ((f32[8,96,48]{1,2,0:T(8,128)}), f32[8,96,48]{1,2,0:T(8,128)S(1)}, u32[]{:S(2)}, u32[]{:S(2)}) async-start(f32[8,96,48]{1,2,0:T(8,128)} %copy.25), calls=%async_computation.8 | async-start | bytes 393216 | tf_op jit(solution)/shard_map/all_to_all | solution.py:11
  289.6 12.6 %all-to-all-start.8 = ((f32[8,96,48]{1,2,0:T(8,128)}), f32[8,96,48]{1,2,0:T(8,128)S(1)}, u32[]{:S(2)}, u32[]{:S(2)}) async-start(f32[8,96,48]{1,2,0:T(8,128)} %broadcast_in_dim.14), calls=%async_computation.9 | async-start | bytes 393216 | tf_op jit(solution)/shard_map/all_to_all | solution.py:19
  302.3 3.7 %copy-start.13 = (f32[128,128]{1,0:T(8,128)S(1)}, f32[128,128]{1,0:T(8,128)}, u32[]{:S(2)}) copy-start(f32[128,128]{1,0:T(8,128)} %fusion.2) | copy-start | bytes 196612
  307.9 2.8 copy-start.4
  307.9 4.4 %copy-start.1 = (bf16[768,1848]{0,1:T(8,128)(2,1)S(1)}, bf16[768,1848]{0,1:T(8,128)(2,1)}, u32[]{:S(2)}) copy-start(bf16[768,1848]{0,1:T(8,128)(2,1)} %param.14) | copy-start | bytes 8515588
Sparse Core Ops, SparseCore 0:
  95.3 76.9 reduce-scatter.1
Sparse Core Ops, SparseCore 1:
  162.3 100.4 all-reduce.1

commit v3 on v2

--- a/solution.py
+++ b/solution.py
@@ -70,6 +70,7 @@
     left_product = jnp.dot(core_left, difference, preferred_element_type=jnp.float32)
     partial_value = jnp.dot(left_product, core_right.astype(jnp.float32).T, precision=highest)
     own_columns = lax.psum_scatter(partial_value, "col", scatter_dimension=1, tiled=True)
+    own_columns = lax.psum(own_columns, "row")
     corange_part = jnp.dot(corange_test, difference, preferred_element_type=jnp.float32)
     corange_sketch = lax.psum(corange_part, "row")
     range_part = jnp.dot(difference, range_test, preferred_element_type=jnp.float32)
@@ -77,12 +78,8 @@
     projected_part = jnp.dot(left_float, range_part, precision=highest)
     projected = scatter_sum(scatter_sum(projected_part, "col", ncol), "row", nrow)
     projected = gather_rows(gather_rows(projected, "row", nrow), "col", ncol)
-    projected, range_part, own_columns = lax.optimization_barrier(
-        (projected, range_part, own_columns)
-    )
+    projected, range_part = lax.optimization_barrier((projected, range_part))
     range_sketch = gather_rows(scatter_sum(range_part, "col", ncol), "col", ncol)
-    range_sketch, own_columns = lax.optimization_barrier((range_sketch, own_columns))
-    own_columns = gather_rows(scatter_sum(own_columns, "row", nrow), "row", nrow)
     gram_matrix = jnp.dot(projected.T, projected, precision=highest)
     right_hand = jnp.dot(projected.T, own_columns, precision=highest)
     core_solution = cholesky_solve(gram_matrix, right_hand)

time: 324 us -> 323 us (level)
  starting transfers between devices: 31.8 us -> 22 us
  waiting for transfers between devices: 77.3 us -> 84.3 us
    psum x1, waiting for transfers between devices: 0.01 us -> 26.4 us  [local(): corange_sketch = lax.psum(corange_part, 'row')]
    all_to_all x3 -> x2, waiting for transfers between devices: 34.7 us -> 15.5 us  [gather_rows(): return lax.all_to_all(tiled, axis, split_axis=0, concat_axis=0, tiled=True)]
    dot_general x1 -> x0, matrix products: 9.69 us -> none  [local(): jnp.dot(left_product, core_right.astype(jnp.float32).T, precision=highest)]
    unnamed x0 -> x1, matrix products: none -> 9.62 us
    all_to_all x3 -> x2, starting transfers between devices: 16.8 us -> 10.9 us  [gather_rows(): return lax.all_to_all(tiled, axis, split_axis=0, concat_axis=0, tiled=True)]
    all_to_all x2 -> x1, starting transfers between devices: 7.28 us -> 3.71 us  [scatter_sum(): got = lax.all_to_all(part, axis, split_axis=0, concat_axis=0, tiled=True)]
    unnamed x35 -> x34, local copies, waits for them, and re-layouts: 13.1 us -> 14.7 us
  transfers between devices with their start and end apart: 8 -> 6, of which waited for: 4 -> 4; matrix products, arithmetic and copies ran while one was open for 35% -> 34% of each run, Pallas kernels for 0% -> 0%
where the time goes in v3:
time: 323 us; the launch traced here: 319 us
  waiting for transfers between devices  84.3 us (26%)
  other arithmetic  78.5 us (24%)
  blocking collectives  43.6 us (13%)
  matrix products  42.7 us (13%)
  local copies, waits for them, and re-layouts  32.9 us (10%)
  starting transfers between devices  22 us (7%)
  between operations  14.9 us (5%)
    all_to_all x1, waiting for transfers between devices, local(): lax.all_to_all(by_target, 'col', split_axis=0, concat_axis=0, tiled=True)  42.3 us
    another operation x9, other arithmetic, cholesky_solve(): low[j, j] = lax.linalg.cholesky(a, symmetrize_input=False)  38.2 us
    all_to_all x2, blocking collectives, scatter_sum(): got = lax.all_to_all(part, axis, split_axis=0, concat_axis=0, tiled=True)  34.8 us
    another operation x6, other arithmetic, cholesky_solve(): lax.linalg.triangular_solve(low[j, j], eye, left_side=True, lower=True)  33.4 us
    psum x1, waiting for transfers between devices, local(): corange_sketch = lax.psum(corange_part, 'row')  26.4 us
    all_to_all x2, waiting for transfers between devices, gather_rows(): return lax.all_to_all(tiled, axis, split_axis=0, concat_axis=0, tiled=True)  15.5 us
    unnamed x34, local copies, waits for them, and re-layouts  14.7 us
    reshape x2, local copies, waits for them, and re-layouts, local(): by_target = adjusted_rows.reshape(height, ncol, width).transpose(1, 0, 2)  13.5 us
  transfers between devices with their start and end apart: 6, of which 4 were waited for; matrix products, arithmetic and copies ran while one was open for 34% of the time, Pallas kernels for 0%

profile of v3, /device:TPU:0, one launch (start us, length us, event | category | flops | bytes accessed | tf_op | source)
XLA Modules:
  0.0 318.9 jit_solution(4376139572267882338)
XLA Ops:
  7.2 8.6 %reshape.50 = bf16[64,16,1848]{2,1,0:T(8,128)(2,1)} reshape(bf16[64,29568]{1,0:T(8,128)(2,1)} %param.9) | data formatting | bytes 7569408 | tf_op jit(solution)/shard_map/reshape | solution.py:64
  15.8 4.9 %copy.24 = bf16[64,16,1848]{2,0,1:T(8,128)(2,1)} copy(bf16[64,16,1848]{2,1,0:T(8,128)(2,1)} %reshape.50) | data formatting | bytes 7569408 | tf_op jit(solution)/shard_map/reshape | solution.py:64
  20.6 7.2 %all-to-all-start = ((bf16[16,64,1848]{2,1,0:T(8,128)(2,1)}), bf16[16,64,1848]{2,1,0:T(8,128)(2,1)}, u32[]{:S(2)}, u32[]{:S(2)}) async-start(bf16[16,64,1848]{2,1,0:T(8,128)(2,1)} %bitcast.87), calls=%async_computation | async-start | bytes 7864320 | tf_op jit(solution)/shard_map/all_to_all | solution.py:65
  27.9 6.6 %copy.16 = bf16[1024,1848]{1,0:T(8,128)(2,1)} copy(bf16[1024,1848]{0,1:T(8,128)(2,1)} %param.10) | data formatting | bytes 7569408 | tf_op args[1]
  34.5 42.3 %all-to-all-done = bf16[16,64,1848]{2,1,0:T(8,128)(2,1)} async-done(((bf16[16,64,1848]{2,1,0:T(8,128)(2,1)}), bf16[16,64,1848]{2,1,0:T(8,128)(2,1)}, u32[]{:S(2)}, u32[]{:S(2)}) %all-to-all-start) | async-done | bytes 3784736 | tf_op jit(solution)/shard_map/all_to_all | solution.py:65
  76.8 4.4 %fusion = bf16[1024,1848]{1,0:T(8,128)(2,1)S(1)} fusion(bf16[1024,1848]{1,0:T(8,128)(2,1)} %copy.16, bf16[16,64,1848]{2,1,0:T(8,128)(2,1)} %all-to-all-done), kind=kLoop, calls=%fused_computation.1 | loop fusion | flops 7569408 | bytes 11354112 | tf_op jit(solution)/shard_map/convert_element_type | solution.py:67
  84.6 3.4 %fusion.22 = f32[1848,768]{1,0:T(8,128)S(1)} fusion(bf16[1024,1848]{1,0:T(8,128)(2,1)S(1)} %fusion, bf16[768,1024]{1,0:T(8,128)(2,1)S(1)} %copy-done.10), kind=kOutput, calls=%fused_computation.50 | convolution fusion | flops 2906652672 | bytes 11034624 | tf_op jit(solution)/shard_map/dot_general | solution.py:70
  88.1 9.6 %convolution_bitcast_fusion.1 = f32[768,768]{1,0:T(8,128)} fusion(f32[1848,768]{1,0:T(8,128)S(1)} %fusion.22, bf16[768,1848]{0,1:T(8,128)(2,1)S(1)} %copy-done), kind=kOutput, calls=%fused_computation.4 | convolution fusion | flops 13079937024 | bytes 10874880
  97.7 5.8 %convolution_bitcast_fusion.2 = f32[768,384]{0,1:T(8,128)S(1)} fusion(f32[1024,384]{1,0:T(8,128)} %fusion.20, bf16[768,1024]{1,0:T(8,128)(2,1)} %param.13), kind=kOutput, calls=%fused_computation.5 | convolution fusion | flops 3623878656 | bytes 4325376 | tf_op jit(solution)/shard_map/dot_general | solution.py:78
  103.8 22.4 %all_to_all.56 = f32[16,48,384]{2,1,0:T(8,128)S(1)} all-to-all(f32[16,48,384]{2,1,0:T(8,128)S(1)} %bitcast.89), channel_id=1, replica_groups=mesh['row'=8,'col'=16] {'col'}, dimensions={0} | all-to-all | bytes 2359296 | tf_op jit(solution)/shard_map/all_to_all | solution.py:11
  126.3 12.4 %all_to_all.57 = f32[8,6,384]{2,1,0:T(8,128)S(1)} all-to-all(f32[8,6,384]{2,1,0:T(8,128)S(1)} %all_to_all.40), channel_id=1, replica_groups=mesh['row'=8,'col'=16] {'row'}, dimensions={0} | all-to-all | bytes 147456 | tf_op jit(solution)/shard_map/all_to_all | solution.py:11
  138.8 8.8 %all_to_all.58 = f32[8,6,384]{2,1,0:T(8,128)S(1)} all-to-all(f32[8,6,384]{2,1,0:T(8,128)S(1)} %broadcast_in_dim.8), channel_id=1, replica_groups=mesh['row'=8,'col'=16] {'row'}, dimensions={0} | all-to-all | bytes 147456 | tf_op jit(solution)/shard_map/all_to_all | solution.py:19
  148.7 3.7 %all-to-all-start.4 = ((f32[16,48,384]{2,1,0:T(8,128)}), f32[16,48,384]{2,1,0:T(8,128)S(1)}, u32[]{:S(2)}, u32[]{:S(2)}) async-start(f32[16,48,384]{2,1,0:T(8,128)} %broadcast_in_dim.10), calls=%async_computation.4 | async-start | bytes 2359296 | tf_op jit(solution)/shard_map/all_to_all | solution.py:19
  152.4 5.9 %convolution_bitcast_fusion = f32[384,1848]{0,1:T(8,128)} fusion(bf16[1024,1848]{1,0:T(8,128)(2,1)} %copy-done.3, bf16[384,1024]{1,0:T(8,128)(2,1)S(1)} %copy-done.14), kind=kOutput, calls=%fused_computation.3 | convolution fusion | flops 1453326336 | bytes 7409664 | tf_op jit(solution)/shard_map/dot_general | solution.py:74
  158.3 15.0 %all-to-all-done.4 = f32[16,48,384]{2,1,0:T(8,128)S(1)} async-done(((f32[16,48,384]{2,1,0:T(8,128)}), f32[16,48,384]{2,1,0:T(8,128)S(1)}, u32[]{:S(2)}, u32[]{:S(2)}) %all-to-all-start.4) | async-done | bytes 1179680 | tf_op jit(solution)/shard_map/all_to_all | solution.py:19
  173.4 3.7 %all-to-all-start.5 = ((f32[16,64,384]{2,1,0:T(8,128)}), f32[16,64,384]{2,1,0:T(8,128)S(1)}, u32[]{:S(2)}, u32[]{:S(2)}) async-start(f32[16,64,384]{2,1,0:T(8,128)} %bitcast.5), calls=%async_computation.5 | async-start | bytes 3145728 | tf_op jit(solution)/shard_map/all_to_all | solution.py:11
  182.4 11.7 %custom-call.10 = f32[128,128]{1,0:T(8,128)S(1)} custom-call(f32[128,128]{1,0:T(8,128)S(1)} %slice.40), custom_call_target="Cholesky" | custom-call | tf_op jit(solution)/shard_map/cholesky/custom-call.1 | solution.py:37
  195.5 9.8 %custom-call.11 = f32[1,128,128]{1,2,0:T(8,128)S(1)} custom-call(f32[1,128,128]{2,1,0:T(8,128)S(1)} %fusion.8), custom_call_target="InvertDiagBlocksLowerTriangular" | custom-call | tf_op jit(solution)/shard_map/triangular_solve/custom-call.0 | solution.py:38
  209.3 12.8 %custom-call.12 = f32[128,128]{1,0:T(8,128)S(1)} custom-call(f32[128,128]{1,0:T(8,128)} %convolution_subtract_fusion.3), custom_call_target="Cholesky" | custom-call | tf_op jit(solution)/shard_map/cholesky/custom-call.1 | solution.py:37
  224.0 11.3 %custom-call.13 = f32[1,128,128]{1,2,0:T(8,128)} custom-call(f32[1,128,128]{2,1,0:T(8,128)} %fusion.9), custom_call_target="InvertDiagBlocksLowerTriangular" | custom-call | tf_op jit(solution)/shard_map/triangular_solve/custom-call.0 | solution.py:38
  240.2 7.2 %all-to-all-start.6 = ((f32[16,64,384]{2,1,0:T(8,128)}), f32[16,64,384]{2,1,0:T(8,128)S(1)}, u32[]{:S(2)}, u32[]{:S(2)}) async-start(f32[16,64,384]{2,1,0:T(8,128)} %broadcast_in_dim.11), calls=%async_computation.6 | async-start | bytes 3145728 | tf_op jit(solution)/shard_map/all_to_all | solution.py:19
  250.6 11.7 %custom-call.14 = f32[128,128]{1,0:T(8,128)S(1)} custom-call(f32[128,128]{1,0:T(8,128)S(1)} %convolution_subtract_fusion), custom_call_target="Cholesky" | custom-call | tf_op jit(solution)/shard_map/cholesky/custom-call.1 | solution.py:37
  263.5 9.8 %custom-call.15 = f32[1,128,128]{1,2,0:T(8,128)S(1)} custom-call(f32[1,128,128]{2,1,0:T(8,128)S(1)} %fusion.10), custom_call_target="InvertDiagBlocksLowerTriangular" | custom-call | tf_op jit(solution)/shard_map/triangular_solve/custom-call.0 | solution.py:38
  274.1 26.4 %all-reduce.3.cloned.1.call-done = (f32[384,1848]{0,1:T(8,128)}, f32[768,48]{1,0:T(8,128)}) async-done(((f32[384,1848]{0,1:T(8,128)}, f32[768,48]{1,0:T(8,128)}), (f32[384,1848]{0,1:T(8,128)}, f32[768,48]{1,0:T(8,128)})) %all-reduce.3.cloned.1.call-update) | async-done | bytes 2986000 | tf_op jit(solution)/shard_map/psum | solution.py:75
  (87 shorter events, 38.7 us)
Async XLA Ops:
  7.2 80.9 %copy-start = (bf16[768,1848]{0,1:T(8,128)(2,1)S(1)}, bf16[768,1848]{0,1:T(8,128)(2,1)}, u32[]{:S(2)}) copy-start(bf16[768,1848]{0,1:T(8,128)(2,1)} %param.14) | copy-start | bytes 8515588
  20.6 56.2 %all-to-all-start = ((bf16[16,64,1848]{2,1,0:T(8,128)(2,1)}), bf16[16,64,1848]{2,1,0:T(8,128)(2,1)}, u32[]{:S(2)}, u32[]{:S(2)}) async-start(bf16[16,64,1848]{2,1,0:T(8,128)(2,1)} %bitcast.87), calls=%async_computation | async-start | bytes 7864320 | tf_op jit(solution)/shard_map/all_to_all | solution.py:65
  27.8 177.5 %reduce-scatter.4.cloned.1.call-start = ((), (), s32[]{:S(2)}) async-start(), calls=%async_computation.8 | async-start | bytes 2506752
  76.8 4.4 %copy-start.13 = (bf16[1848,384]{1,0:T(8,128)(2,1)S(1)}, bf16[1848,384]{1,0:T(8,128)(2,1)}, u32[]{:S(2)}) copy-start(bf16[1848,384]{1,0:T(8,128)(2,1)} %param.11) | copy-start | bytes 4257796
  81.2 3.4 %copy-start.3 = (bf16[1024,1848]{1,0:T(8,128)(2,1)}, bf16[1024,1848]{1,0:T(8,128)(2,1)S(1)}, u32[]{:S(2)}) copy-start(bf16[1024,1848]{1,0:T(8,128)(2,1)S(1)} %fusion) | copy-start | bytes 11354116
  81.2 3.4 %copy-start.10 = (bf16[768,1024]{1,0:T(8,128)(2,1)S(1)}, bf16[768,1024]{1,0:T(8,128)(2,1)}, u32[]{:S(2)}) copy-start(bf16[768,1024]{1,0:T(8,128)(2,1)} %param.13) | copy-start | bytes 4718596
  126.3 26.1 %copy-start.14 = (bf16[384,1024]{1,0:T(8,128)(2,1)S(1)}, bf16[384,1024]{1,0:T(8,128)(2,1)}, u32[]{:S(2)}) copy-start(bf16[384,1024]{1,0:T(8,128)(2,1)} %param.12) | copy-start | bytes 2359300
  148.7 24.7 %all-to-all-start.4 = ((f32[16,48,384]{2,1,0:T(8,128)}), f32[16,48,384]{2,1,0:T(8,128)S(1)}, u32[]{:S(2)}, u32[]{:S(2)}) async-start(f32[16,48,384]{2,1,0:T(8,128)} %broadcast_in_dim.10), calls=%async_computation.4 | async-start | bytes 2359296 | tf_op jit(solution)/shard_map/all_to_all | solution.py:19
  173.4 64.0 %all-to-all-start.5 = ((f32[16,64,384]{2,1,0:T(8,128)}), f32[16,64,384]{2,1,0:T(8,128)S(1)}, u32[]{:S(2)}, u32[]{:S(2)}) async-start(f32[16,64,384]{2,1,0:T(8,128)} %bitcast.5), calls=%async_computation.5 | async-start | bytes 3145728 | tf_op jit(solution)/shard_map/all_to_all | solution.py:11
  177.1 123.4 %all-reduce.3.cloned.1.call-start = ((), (), s32[]{:S(2)}) async-start(), calls=%async_computation.9 | async-start | bytes 6463488 | tf_op jit(solution)/shard_map/psum | solution.py:75
  181.6 0.8 copy-start.5
  182.4 25.7 %copy-start.6 = (f32[384,384]{1,0:T(8,128)S(1)}, f32[384,384]{1,0:T(8,128)}, u32[]{:S(2)}) copy-start(f32[384,384]{1,0:T(8,128)} %copy-done.5) | copy-start | bytes 1769476
  207.5 0.6 copy-start.7
  240.2 33.9 %all-to-all-start.6 = ((f32[16,64,384]{2,1,0:T(8,128)}), f32[16,64,384]{2,1,0:T(8,128)S(1)}, u32[]{:S(2)}, u32[]{:S(2)}) async-start(f32[16,64,384]{2,1,0:T(8,128)} %broadcast_in_dim.11), calls=%async_computation.6 | async-start | bytes 3145728 | tf_op jit(solution)/shard_map/all_to_all | solution.py:19
  248.5 1.4 copy-start.11
  249.7 0.6 copy-start.8
  250.5 53.4 %copy-start.12 = (f32[128,128]{1,0:T(8,128)S(1)}, f32[128,128]{1,0:T(8,128)}, u32[]{:S(2)}) copy-start(f32[128,128]{1,0:T(8,128)} %copy-done.11) | copy-start | bytes 196612
  250.6 53.7 %copy-start.9 = (f32[128,128]{1,0:T(8,128)S(1)}, f32[128,128]{1,0:T(8,128)}, u32[]{:S(2)}) copy-start(f32[128,128]{1,0:T(8,128)} %copy-done.8) | copy-start | bytes 196612
  274.1 28.3 %copy-start.2 = (f32[16,64,384]{2,1,0:T(8,128)}, f32[16,64,384]{2,1,0:T(8,128)S(1)}, u32[]{:S(2)}) copy-start(f32[16,64,384]{2,1,0:T(8,128)S(1)} %all-to-all-done.6) | copy-start | bytes 4718596
  303.5 6.6 %copy-start.4 = (f32[384,1848]{0,1:T(8,128)S(1)}, f32[384,1848]{0,1:T(8,128)}, u32[]{:S(2)}) copy-start(f32[384,1848]{0,1:T(8,128)} %get-tuple-element.15) | copy-start | bytes 8515588
  307.3 4.4 %copy-start.1 = (bf16[768,1848]{0,1:T(8,128)(2,1)S(1)}, bf16[768,1848]{0,1:T(8,128)(2,1)}, u32[]{:S(2)}) copy-start(bf16[768,1848]{0,1:T(8,128)(2,1)} %param.14) | copy-start | bytes 8515588
Sparse Core Ops, SparseCore 0:
  97.8 76.5 reduce-scatter.3
  207.3 93.0 all-reduce.2

commit v4 on v3

--- a/solution.py
+++ b/solution.py
@@ -70,7 +70,8 @@
     left_product = jnp.dot(core_left, difference, preferred_element_type=jnp.float32)
     partial_value = jnp.dot(left_product, core_right.astype(jnp.float32).T, precision=highest)
     own_columns = lax.psum_scatter(partial_value, "col", scatter_dimension=1, tiled=True)
-    own_columns = lax.psum(own_columns, "row")
+    own_columns = lax.psum_scatter(own_columns, "row", scatter_dimension=0, tiled=True)
+    own_columns = lax.all_gather(own_columns, "row", axis=0, tiled=True)
     corange_part = jnp.dot(corange_test, difference, preferred_element_type=jnp.float32)
     corange_sketch = lax.psum(corange_part, "row")
     range_part = jnp.dot(difference, range_test, preferred_element_type=jnp.float32)

time: 323 us -> 359 us (1.11)
  blocking collectives: 43.6 us -> 99.9 us
  waiting for transfers between devices: 84.3 us -> 69.9 us
  other arithmetic: 78.5 us -> 74.7 us
    all_gather x0 -> x1, blocking collectives: none -> 57.1 us  [local(): own_columns = lax.all_gather(own_columns, 'row', axis=0, tiled=True)]
    psum x1, waiting for transfers between devices: 26.4 us -> 0.01 us  [local(): corange_sketch = lax.psum(corange_part, 'row')]
    reduce_scatter x0 -> x1, waiting for transfers between devices: none -> 16 us  [local(): lax.psum_scatter(partial_value, 'col', scatter_dimension=1, tiled=True)]
    all_to_all x2, waiting for transfers between devices: 15.5 us -> 0.01 us  [gather_rows(): return lax.all_to_all(tiled, axis, split_axis=0, concat_axis=0, tiled=True)]
    all_to_all x1, waiting for transfers between devices: 0.01 us -> 11.1 us  [scatter_sum(): got = lax.all_to_all(part, axis, split_axis=0, concat_axis=0, tiled=True)]
    dot_general x0 -> x1, matrix products: none -> 9.68 us  [local(): jnp.dot(left_product, core_right.astype(jnp.float32).T, precision=highest)]
    unnamed x1 -> x0, matrix products: 9.62 us -> none
  transfers between devices with their start and end apart: 6 -> 7, of which waited for: 4 -> 3; matrix products, arithmetic and copies ran while one was open for 34% -> 31% of each run, Pallas kernels for 0% -> 0%
where the time goes in v4:
time: 359 us; the launch traced here: 353 us
  blocking collectives  99.9 us (28%)
  other arithmetic  74.7 us (21%)
  waiting for transfers between devices  69.9 us (19%)
  matrix products  40.2 us (11%)
  local copies, waits for them, and re-layouts  31.8 us (9%)
  starting transfers between devices  22.4 us (6%)
  between operations  14.4 us (4%)
    all_gather x1, blocking collectives, local(): own_columns = lax.all_gather(own_columns, 'row', axis=0, tiled=True)  57.1 us
    all_to_all x1, waiting for transfers between devices, local(): lax.all_to_all(by_target, 'col', split_axis=0, concat_axis=0, tiled=True)  42.6 us
    another operation x9, other arithmetic, cholesky_solve(): low[j, j] = lax.linalg.cholesky(a, symmetrize_input=False)  37.4 us
    all_to_all x2, blocking collectives, scatter_sum(): got = lax.all_to_all(part, axis, split_axis=0, concat_axis=0, tiled=True)  33.9 us
    another operation x6, other arithmetic, cholesky_solve(): lax.linalg.triangular_solve(low[j, j], eye, left_side=True, lower=True)  32 us
    reduce_scatter x1, waiting for transfers between devices, local(): lax.psum_scatter(partial_value, 'col', scatter_dimension=1, tiled=True)  16 us
    unnamed x34, local copies, waits for them, and re-layouts  15.2 us
    reshape x2, local copies, waits for them, and re-layouts, local(): by_target = adjusted_rows.reshape(height, ncol, width).transpose(1, 0, 2)  13.5 us
  transfers between devices with their start and end apart: 7, of which 3 were waited for; matrix products, arithmetic and copies ran while one was open for 31% of the time, Pallas kernels for 0%

profile of v4, /device:TPU:0, one launch (start us, length us, event | category | flops | bytes accessed | tf_op | source)
XLA Modules:
  0.0 353.2 jit_solution(10861776591265147233)
XLA Ops:
  7.2 8.6 %reshape.50 = bf16[64,16,1848]{2,1,0:T(8,128)(2,1)} reshape(bf16[64,29568]{1,0:T(8,128)(2,1)} %param.9) | data formatting | bytes 7569408 | tf_op jit(solution)/shard_map/reshape | solution.py:64
  15.8 4.9 %copy.24 = bf16[64,16,1848]{2,0,1:T(8,128)(2,1)} copy(bf16[64,16,1848]{2,1,0:T(8,128)(2,1)} %reshape.50) | data formatting | bytes 7569408 | tf_op jit(solution)/shard_map/reshape | solution.py:64
  20.6 7.2 %all-to-all-start = ((bf16[16,64,1848]{2,1,0:T(8,128)(2,1)}), bf16[16,64,1848]{2,1,0:T(8,128)(2,1)}, u32[]{:S(2)}, u32[]{:S(2)}) async-start(bf16[16,64,1848]{2,1,0:T(8,128)(2,1)} %bitcast.88), calls=%async_computation | async-start | bytes 7864320 | tf_op jit(solution)/shard_map/all_to_all | solution.py:65
  27.9 6.3 %copy.17 = bf16[1024,1848]{1,0:T(8,128)(2,1)} copy(bf16[1024,1848]{0,1:T(8,128)(2,1)} %param.10) | data formatting | bytes 7569408 | tf_op args[1]
  34.2 42.6 %all-to-all-done = bf16[16,64,1848]{2,1,0:T(8,128)(2,1)} async-done(((bf16[16,64,1848]{2,1,0:T(8,128)(2,1)}), bf16[16,64,1848]{2,1,0:T(8,128)(2,1)}, u32[]{:S(2)}, u32[]{:S(2)}) %all-to-all-start) | async-done | bytes 3784736 | tf_op jit(solution)/shard_map/all_to_all | solution.py:65
  76.8 4.4 %fusion = bf16[1024,1848]{1,0:T(8,128)(2,1)S(1)} fusion(bf16[1024,1848]{1,0:T(8,128)(2,1)} %copy.17, bf16[16,64,1848]{2,1,0:T(8,128)(2,1)} %all-to-all-done), kind=kLoop, calls=%fused_computation.1 | loop fusion | flops 7569408 | bytes 11354112 | tf_op jit(solution)/shard_map/convert_element_type | solution.py:67
  84.7 9.7 %fusion.23 = f32[768,768]{0,1:T(8,128)} fusion(f32[1848,768]{1,0:T(8,128)S(1)} %fusion.22, bf16[768,1848]{0,1:T(8,128)(2,1)S(1)} %copy-done), kind=kOutput, calls=%fused_computation.50 | convolution fusion | flops 13079937024 | bytes 10874880 | tf_op jit(solution)/shard_map/dot_general | solution.py:71
  95.7 5.6 %fusion.20 = f32[1024,384]{1,0:T(8,128)} fusion(bf16[1024,1848]{1,0:T(8,128)(2,1)} %copy-done.2, bf16[1848,384]{1,0:T(8,128)(2,1)S(1)} %copy-done.12), kind=kOutput, calls=%fused_computation.47 | convolution fusion | flops 1453326336 | bytes 6776832 | tf_op jit(solution)/shard_map/dot_general | solution.py:77
  101.3 5.3 %convolution_bitcast_fusion.1 = f32[768,384]{0,1:T(8,128)S(1)} fusion(f32[1024,384]{1,0:T(8,128)} %fusion.20, bf16[768,1024]{1,0:T(8,128)(2,1)S(1)} %copy-done.9), kind=kOutput, calls=%fused_computation.4 | convolution fusion | flops 3623878656 | bytes 4325376 | tf_op jit(solution)/shard_map/dot_general | solution.py:79
  107.0 22.3 %all_to_all.56 = f32[16,48,384]{2,1,0:T(8,128)S(1)} all-to-all(f32[16,48,384]{2,1,0:T(8,128)S(1)} %bitcast.89), channel_id=1, replica_groups=mesh['row'=8,'col'=16] {'col'}, dimensions={0} | all-to-all | bytes 2359296 | tf_op jit(solution)/shard_map/all_to_all | solution.py:11
  129.4 11.6 %all_to_all.57 = f32[8,6,384]{2,1,0:T(8,128)S(1)} all-to-all(f32[8,6,384]{2,1,0:T(8,128)S(1)} %all_to_all.40), channel_id=1, replica_groups=mesh['row'=8,'col'=16] {'row'}, dimensions={0} | all-to-all | bytes 147456 | tf_op jit(solution)/shard_map/all_to_all | solution.py:11
  141.0 8.9 %all_to_all.58 = f32[8,6,384]{2,1,0:T(8,128)S(1)} all-to-all(f32[8,6,384]{2,1,0:T(8,128)S(1)} %broadcast_in_dim.8), channel_id=1, replica_groups=mesh['row'=8,'col'=16] {'row'}, dimensions={0} | all-to-all | bytes 147456 | tf_op jit(solution)/shard_map/all_to_all | solution.py:19
  154.8 16.0 %reduce-scatter.5.cloned.1.call-done = f32[768,48]{0,1:T(8,128)} async-done(((f32[768,768]{0,1:T(8,128)}), f32[768,48]{0,1:T(8,128)}) %reduce-scatter.5.cloned.1.call-update) | async-done | bytes 147472 | tf_op jit(solution)/shard_map/reduce_scatter | solution.py:72
  173.3 5.9 %convolution_bitcast_fusion = f32[384,1848]{0,1:T(8,128)} fusion(bf16[1024,1848]{1,0:T(8,128)(2,1)} %copy-done.2, bf16[384,1024]{1,0:T(8,128)(2,1)S(1)} %copy-done.13), kind=kOutput, calls=%fused_computation.3 | convolution fusion | flops 1453326336 | bytes 7409664 | tf_op jit(solution)/shard_map/dot_general | solution.py:75
  181.6 11.7 %custom-call.10 = f32[128,128]{1,0:T(8,128)S(1)} custom-call(f32[128,128]{1,0:T(8,128)S(1)} %slice.40), custom_call_target="Cholesky" | custom-call | tf_op jit(solution)/shard_map/cholesky/custom-call.1 | solution.py:37
  194.6 9.8 %custom-call.11 = f32[1,128,128]{1,2,0:T(8,128)S(1)} custom-call(f32[1,128,128]{2,1,0:T(8,128)S(1)} %fusion.8), custom_call_target="InvertDiagBlocksLowerTriangular" | custom-call | tf_op jit(solution)/shard_map/triangular_solve/custom-call.0 | solution.py:38
  205.6 11.9 %custom-call.12 = f32[128,128]{1,0:T(8,128)S(1)} custom-call(f32[128,128]{1,0:T(8,128)S(1)} %convolution_subtract_fusion.3), custom_call_target="Cholesky" | custom-call | tf_op jit(solution)/shard_map/cholesky/custom-call.1 | solution.py:37
  218.8 10.4 %custom-call.13 = f32[1,128,128]{1,2,0:T(8,128)} custom-call(f32[1,128,128]{2,1,0:T(8,128)S(1)} %fusion.9), custom_call_target="InvertDiagBlocksLowerTriangular" | custom-call | tf_op jit(solution)/shard_map/triangular_solve/custom-call.0 | solution.py:38
  230.1 6.4 %all-to-all-start.5 = ((f32[16,64,384]{2,1,0:T(8,128)}), f32[16,64,384]{2,1,0:T(8,128)S(1)}, u32[]{:S(2)}, u32[]{:S(2)}) async-start(f32[16,64,384]{2,1,0:T(8,128)} %bitcast.5), calls=%async_computation.5 | async-start | bytes 3145728 | tf_op jit(solution)/shard_map/all_to_all | solution.py:11
  239.7 11.7 %custom-call.14 = f32[128,128]{1,0:T(8,128)S(1)} custom-call(f32[128,128]{1,0:T(8,128)S(1)} %convolution_subtract_fusion), custom_call_target="Cholesky" | custom-call | tf_op jit(solution)/shard_map/cholesky/custom-call.1 | solution.py:37
  252.8 9.8 %custom-call.15 = f32[1,128,128]{1,2,0:T(8,128)S(1)} custom-call(f32[1,128,128]{2,1,0:T(8,128)S(1)} %fusion.10), custom_call_target="InvertDiagBlocksLowerTriangular" | custom-call | tf_op jit(solution)/shard_map/triangular_solve/custom-call.0 | solution.py:38
  262.9 11.1 %all-to-all-done.5 = f32[16,64,384]{2,1,0:T(8,128)S(1)} async-done(((f32[16,64,384]{2,1,0:T(8,128)}), f32[16,64,384]{2,1,0:T(8,128)S(1)}, u32[]{:S(2)}, u32[]{:S(2)}) %all-to-all-start.5) | async-done | bytes 1572896 | tf_op jit(solution)/shard_map/all_to_all | solution.py:11
  275.4 4.5 %all-to-all-start.6 = ((f32[16,64,384]{2,1,0:T(8,128)}), f32[16,64,384]{2,1,0:T(8,128)}, u32[]{:S(2)}, u32[]{:S(2)}) async-start(f32[16,64,384]{2,1,0:T(8,128)} %broadcast_in_dim.11), calls=%async_computation.6 | async-start | bytes 3145728 | tf_op jit(solution)/shard_map/all_to_all | solution.py:19
  280.9 57.1 %all-gather = f32[8,96,48]{1,2,0:T(8,128)S(1)} all-gather(f32[1,96,48]{1,2,0:T(8,128)S(1)} %bitcast.90), channel_id=1, replica_groups=mesh['row'=8,'col'=16] {'row'}, dimensions={0}, use_global_device_ids=true | all-gather | bytes 165888 | tf_op jit(solution)/shard_map/all_gather | solution.py:74
  (92 shorter events, 35.0 us)
Async XLA Ops:
  7.2 77.5 %copy-start = (bf16[768,1848]{0,1:T(8,128)(2,1)S(1)}, bf16[768,1848]{0,1:T(8,128)(2,1)}, u32[]{:S(2)}) copy-start(bf16[768,1848]{0,1:T(8,128)(2,1)} %param.14) | copy-start | bytes 8515588
  20.6 56.2 %all-to-all-start = ((bf16[16,64,1848]{2,1,0:T(8,128)(2,1)}), bf16[16,64,1848]{2,1,0:T(8,128)(2,1)}, u32[]{:S(2)}, u32[]{:S(2)}) async-start(bf16[16,64,1848]{2,1,0:T(8,128)(2,1)} %bitcast.88), calls=%async_computation | async-start | bytes 7864320 | tf_op jit(solution)/shard_map/all_to_all | solution.py:65
  27.8 143.0 %reduce-scatter.5.cloned.1.call-start = ((), (), s32[]{:S(2)}) async-start(), calls=%async_computation.10 | async-start | bytes 2506752 | tf_op jit(solution)/shard_map/reduce_scatter | solution.py:72
  76.8 4.4 %copy-start.8 = (bf16[768,1024]{1,0:T(8,128)(2,1)S(1)}, bf16[768,1024]{1,0:T(8,128)(2,1)}, u32[]{:S(2)}) copy-start(bf16[768,1024]{1,0:T(8,128)(2,1)} %param.13) | copy-start | bytes 4718596
  81.2 3.4 copy-start.2
  94.3 1.4 copy-start.12
  95.7 5.6 %copy-start.9 = (bf16[768,1024]{1,0:T(8,128)(2,1)S(1)}, bf16[768,1024]{1,0:T(8,128)(2,1)}, u32[]{:S(2)}) copy-start(bf16[768,1024]{1,0:T(8,128)(2,1)} %param.13) | copy-start | bytes 4718596
  149.9 23.3 %copy-start.13 = (bf16[384,1024]{1,0:T(8,128)(2,1)S(1)}, bf16[384,1024]{1,0:T(8,128)(2,1)}, u32[]{:S(2)}) copy-start(bf16[384,1024]{1,0:T(8,128)(2,1)} %param.12) | copy-start | bytes 2359300
  151.1 28.1 %all-to-all-start.4 = ((f32[16,48,384]{2,1,0:T(8,128)}), f32[16,48,384]{2,1,0:T(8,128)S(1)}, u32[]{:S(2)}, u32[]{:S(2)}) async-start(f32[16,48,384]{2,1,0:T(8,128)} %broadcast_in_dim.10), calls=%async_computation.4 | async-start | bytes 2359296 | tf_op jit(solution)/shard_map/all_to_all | solution.py:19
  154.8 125.2 %reduce-scatter.7.cloned.1.call-start = ((), (), s32[]{:S(2)}) async-start(), calls=%async_computation.11 | async-start | bytes 442368
  172.7 169.4 %all-reduce.2.cloned.1.call-start = ((), (), s32[]{:S(2)}) async-start(), calls=%async_computation.9 | async-start | bytes 5677056 | tf_op jit(solution)/shard_map/psum | solution.py:76
  204.8 25.4 %copy-start.4 = (f32[128,128]{1,0:T(8,128)}, f32[128,128]{1,0:T(8,128)S(1)}, u32[]{:S(2)}) copy-start(f32[128,128]{1,0:T(8,128)S(1)} %fusion.6) | copy-start | bytes 196612
  230.1 43.9 %all-to-all-start.5 = ((f32[16,64,384]{2,1,0:T(8,128)}), f32[16,64,384]{2,1,0:T(8,128)S(1)}, u32[]{:S(2)}, u32[]{:S(2)}) async-start(f32[16,64,384]{2,1,0:T(8,128)} %bitcast.5), calls=%async_computation.5 | async-start | bytes 3145728 | tf_op jit(solution)/shard_map/all_to_all | solution.py:11
  237.6 1.4 copy-start.10
  238.8 0.6 copy-start.6
  275.4 63.5 %copy-start.5 = (f32[128,128]{1,0:T(8,128)S(1)}, f32[128,128]{1,0:T(8,128)}, u32[]{:S(2)}) copy-start(f32[128,128]{1,0:T(8,128)} %copy-done.4) | copy-start | bytes 196612
  275.4 64.0 %copy-start.11 = (f32[128,128]{1,0:T(8,128)S(1)}, f32[128,128]{1,0:T(8,128)}, u32[]{:S(2)}) copy-start(f32[128,128]{1,0:T(8,128)} %copy-done.10) | copy-start | bytes 196612
  275.4 64.4 %copy-start.7 = (f32[128,128]{1,0:T(8,128)S(1)}, f32[128,128]{1,0:T(8,128)}, u32[]{:S(2)}) copy-start(f32[128,128]{1,0:T(8,128)} %copy-done.6) | copy-start | bytes 196612
  275.4 66.6 %all-to-all-start.6 = ((f32[16,64,384]{2,1,0:T(8,128)}), f32[16,64,384]{2,1,0:T(8,128)}, u32[]{:S(2)}, u32[]{:S(2)}) async-start(f32[16,64,384]{2,1,0:T(8,128)} %broadcast_in_dim.11), calls=%async_computation.6 | async-start | bytes 3145728 | tf_op jit(solution)/shard_map/all_to_all | solution.py:19
  342.1 2.8 copy-start.3
  342.1 4.4 %copy-start.1 = (bf16[768,1848]{0,1:T(8,128)(2,1)S(1)}, bf16[768,1848]{0,1:T(8,128)(2,1)}, u32[]{:S(2)}) copy-start(bf16[768,1848]{0,1:T(8,128)(2,1)} %param.14) | copy-start | bytes 8515588
Sparse Core Ops, SparseCore 0:
  94.5 76.3 reduce-scatter.4
  173.2 38.0 reduce-scatter.6
  214.5 112.8 all-reduce.1

commit v5 on v3

--- a/solution.py
+++ b/solution.py
@@ -2,6 +2,8 @@
 import jax.numpy as jnp
 from jax import lax
 from jax.sharding import PartitionSpec as P
+from jax.experimental import pallas as pl
+from jax.experimental.pallas import tpu as pltpu
 
 S = 768
 
@@ -17,6 +19,20 @@
         groups * chunk.shape[0], *chunk.shape[1:]
     )
     return lax.all_to_all(tiled, axis, split_axis=0, concat_axis=0, tiled=True)
+
+
+def split_columns(rows, parts):
+    height, width = rows.shape[0], rows.shape[1] // parts
+
+    def kernel(x_ref, o_ref):
+        for j in range(parts):
+            o_ref[j] = x_ref[:, j * width:(j + 1) * width]
+
+    return pl.pallas_call(
+        kernel,
+        out_shape=jax.ShapeDtypeStruct((parts, height, width), rows.dtype),
+        compiler_params=pltpu.CompilerParams(vmem_limit_bytes=48 * 1024 * 1024),
+    )(rows)
 
 
 def dot_hi(a, b):
@@ -61,7 +77,7 @@
     ncol = lax.axis_size("col")
     nrow = lax.axis_size("row")
     height, width = adjusted_rows.shape[0], adjusted_rows.shape[1] // ncol
-    by_target = adjusted_rows.reshape(height, ncol, width).transpose(1, 0, 2)
+    by_target = split_columns(adjusted_rows, ncol)
     adjusted_block = lax.all_to_all(by_target, "col", split_axis=0, concat_axis=0, tiled=True)
     adjusted_block = adjusted_block.reshape(ncol * height, width)
     difference = (adjusted_block.astype(jnp.float32) - base_weight.astype(jnp.float32)).astype(

time: 323 us -> 338 us (1.046)
  blocking collectives: 43.6 us -> 99.3 us
  waiting for transfers between devices: 84.3 us -> 52 us
  local copies, waits for them, and re-layouts: 32.9 us -> 22.6 us
  starting transfers between devices: 22 us -> 15.5 us
  other arithmetic: 78.5 us -> 82.5 us
    all_to_all x0 -> x1, blocking collectives: none -> 56 us  [local(): lax.all_to_all(by_target, 'col', split_axis=0, concat_axis=0, tiled=True)]
    all_to_all x1 -> x0, waiting for transfers between devices: 42.3 us -> none  [local(): lax.all_to_all(by_target, 'col', split_axis=0, concat_axis=0, tiled=True)]
    reshape x2 -> x0, local copies, waits for them, and re-layouts: 13.5 us -> none  [local(): by_target = adjusted_rows.reshape(height, ncol, width).transpose(1, 0, 2)]
    convert_element_type x0 -> x1, local copies, waits for them, and re-layouts: none -> 9.16 us  [local(): adjusted_block.astype(jnp.float32) - base_weight.astype(jnp.float32)]
    psum x1, waiting for transfers between devices: 26.4 us -> 33.8 us  [local(): corange_sketch = lax.psum(corange_part, 'row')]
    all_to_all x1 -> x0, starting transfers between devices: 7.19 us -> none  [local(): lax.all_to_all(by_target, 'col', split_axis=0, concat_axis=0, tiled=True)]
    unnamed x34 -> x31, local copies, waits for them, and re-layouts: 14.7 us -> 9.46 us
    convert_element_type x0 -> x1, other arithmetic: none -> 3.87 us  [local(): adjusted_block.astype(jnp.float32) - base_weight.astype(jnp.float32)]
  transfers between devices with their start and end apart: 6 -> 5, of which waited for: 4 -> 3; matrix products, arithmetic and copies ran while one was open for 34% -> 29% of each run, Pallas kernels for 0% -> 0%
where the time goes in v5:
time: 338 us; the launch traced here: 334 us
  blocking collectives  99.3 us (29%)
  other arithmetic  82.5 us (24%)
  waiting for transfers between devices  52 us (15%)
  matrix products  44.5 us (13%)
  local copies, waits for them, and re-layouts  22.6 us (7%)
  starting transfers between devices  15.5 us (5%)
  between operations  14.7 us (4%)
    all_to_all x1, blocking collectives, local(): lax.all_to_all(by_target, 'col', split_axis=0, concat_axis=0, tiled=True)  56 us
    another operation x9, other arithmetic, cholesky_solve(): low[j, j] = lax.linalg.cholesky(a, symmetrize_input=False)  38 us
    all_to_all x2, blocking collectives, scatter_sum(): got = lax.all_to_all(part, axis, split_axis=0, concat_axis=0, tiled=True)  34.5 us
    psum x1, waiting for transfers between devices, local(): corange_sketch = lax.psum(corange_part, 'row')  33.8 us
    another operation x6, other arithmetic, cholesky_solve(): lax.linalg.triangular_solve(low[j, j], eye, left_side=True, lower=True)  33.4 us
    all_to_all x2, waiting for transfers between devices, gather_rows(): return lax.all_to_all(tiled, axis, split_axis=0, concat_axis=0, tiled=True)  18.2 us
    all_to_all x2, starting transfers between devices, gather_rows(): return lax.all_to_all(tiled, axis, split_axis=0, concat_axis=0, tiled=True)  11.5 us
    dot_general x19, matrix products, dot_hi(): return jnp.dot(a, b, precision=lax.Precision.HIGHEST)  10.6 us
  transfers between devices with their start and end apart: 5, of which 3 were waited for; matrix products, arithmetic and copies ran while one was open for 29% of the time, Pallas kernels for 0%

profile of v5, /device:TPU:0, one launch (start us, length us, event | category | flops | bytes accessed | tf_op | source)
XLA Modules:
  0.0 334.0 jit_solution(12315351699577876263)
XLA Ops:
  12.4 56.0 %all_to_all.56 = bf16[16,64,1848]{2,1,0:T(8,128)(2,1)S(1)} all-to-all(bf16[16,64,1848]{2,1,0:T(8,128)(2,1)} %shard_map.85), channel_id=1, replica_groups=mesh['row'=8,'col'=16] {'col'}, dimensions={0} | all-to-all | bytes 7569408 | tf_op jit(solution)/shard_map/all_to_all | solution.py:81
  68.4 3.9 %bitcast_convert_fusion = f32[1024,1848]{1,0:T(8,128)} fusion(bf16[16,64,1848]{2,1,0:T(8,128)(2,1)S(1)} %all_to_all.56), kind=kLoop, calls=%fused_computation.1 | loop fusion | flops 1892352 | bytes 11354112 | tf_op jit(solution)/shard_map/convert_element_type | solution.py:83
  72.3 9.2 %copy.14 = f32[1024,1848]{0,1:T(8,128)} copy(f32[1024,1848]{1,0:T(8,128)} %bitcast_convert_fusion) | data formatting | bytes 15138816 | tf_op jit(solution)/shard_map/convert_element_type | solution.py:83
  81.4 5.8 %subtract_convert_fusion = bf16[1024,1848]{0,1:T(8,128)(2,1)S(1)} fusion(f32[1024,1848]{0,1:T(8,128)} %copy.14, bf16[1024,1848]{0,1:T(8,128)(2,1)} %param.10), kind=kLoop, calls=%fused_computation | loop fusion | flops 5677056 | bytes 15138816 | tf_op jit(solution)/shard_map/convert_element_type | solution.py:83
  87.2 3.5 %fusion.19 = f32[1024,384]{1,0:T(8,128)} fusion(bf16[1024,1848]{0,1:T(8,128)(2,1)S(1)} %subtract_convert_fusion, bf16[1848,384]{1,0:T(8,128)(2,1)S(1)} %copy-done.12), kind=kOutput, calls=%fused_computation.47 | convolution fusion | flops 1453326336 | bytes 6776832 | tf_op jit(solution)/shard_map/dot_general | solution.py:92
  90.7 3.4 %fusion.21 = f32[1848,768]{1,0:T(8,128)S(1)} fusion(bf16[1024,1848]{0,1:T(8,128)(2,1)S(1)} %subtract_convert_fusion, bf16[768,1024]{1,0:T(8,128)(2,1)S(1)} %copy-done.9), kind=kOutput, calls=%fused_computation.49 | convolution fusion | flops 2906652672 | bytes 11034624 | tf_op jit(solution)/shard_map/dot_general | solution.py:86
  94.1 9.7 %convolution_bitcast_fusion.1 = f32[768,768]{1,0:T(8,128)} fusion(f32[1848,768]{1,0:T(8,128)S(1)} %fusion.21, bf16[768,1848]{0,1:T(8,128)(2,1)S(1)} %copy-done), kind=kOutput, calls=%fused_computation.3 | convolution fusion | flops 13079937024 | bytes 10874880
  103.9 5.8 %convolution_bitcast_fusion.2 = f32[768,384]{0,1:T(8,128)S(1)} fusion(f32[1024,384]{1,0:T(8,128)} %fusion.19, bf16[768,1024]{1,0:T(8,128)(2,1)} %param.13), kind=kOutput, calls=%fused_computation.4 | convolution fusion | flops 3623878656 | bytes 4325376 | tf_op jit(solution)/shard_map/dot_general | solution.py:94
  110.0 22.0 %all_to_all.57 = f32[16,48,384]{2,1,0:T(8,128)S(1)} all-to-all(f32[16,48,384]{2,1,0:T(8,128)S(1)} %bitcast.85), channel_id=1, replica_groups=mesh['row'=8,'col'=16] {'col'}, dimensions={0} | all-to-all | bytes 2359296 | tf_op jit(solution)/shard_map/all_to_all | solution.py:13
  132.1 12.4 %all_to_all.58 = f32[8,6,384]{2,1,0:T(8,128)S(1)} all-to-all(f32[8,6,384]{2,1,0:T(8,128)S(1)} %all_to_all.40), channel_id=1, replica_groups=mesh['row'=8,'col'=16] {'row'}, dimensions={0} | all-to-all | bytes 147456 | tf_op jit(solution)/shard_map/all_to_all | solution.py:13
  144.6 8.8 %all_to_all.59 = f32[8,6,384]{2,1,0:T(8,128)S(1)} all-to-all(f32[8,6,384]{2,1,0:T(8,128)S(1)} %broadcast_in_dim.8), channel_id=1, replica_groups=mesh['row'=8,'col'=16] {'row'}, dimensions={0} | all-to-all | bytes 147456 | tf_op jit(solution)/shard_map/all_to_all | solution.py:21
  154.6 4.2 %all-to-all-start.4 = ((f32[16,48,384]{2,1,0:T(8,128)}), f32[16,48,384]{2,1,0:T(8,128)S(1)}, u32[]{:S(2)}, u32[]{:S(2)}) async-start(f32[16,48,384]{2,1,0:T(8,128)} %broadcast_in_dim.10), calls=%async_computation.4 | async-start | bytes 2359296 | tf_op jit(solution)/shard_map/all_to_all | solution.py:21
  158.7 5.8 %convolution_bitcast_fusion = f32[384,1848]{0,1:T(8,128)} fusion(bf16[1024,1848]{0,1:T(8,128)(2,1)} %copy-done.4, bf16[384,1024]{1,0:T(8,128)(2,1)S(1)} %copy-done.13), kind=kOutput, calls=%fused_computation.2 | convolution fusion | flops 1453326336 | bytes 7409664 | tf_op jit(solution)/shard_map/dot_general | solution.py:90
  164.5 15.1 %all-to-all-done.4 = f32[16,48,384]{2,1,0:T(8,128)S(1)} async-done(((f32[16,48,384]{2,1,0:T(8,128)}), f32[16,48,384]{2,1,0:T(8,128)S(1)}, u32[]{:S(2)}, u32[]{:S(2)}) %all-to-all-start.4) | async-done | bytes 1179680 | tf_op jit(solution)/shard_map/all_to_all | solution.py:21
  182.0 11.7 %custom-call.10 = f32[128,128]{1,0:T(8,128)S(1)} custom-call(f32[128,128]{1,0:T(8,128)S(1)} %slice.40), custom_call_target="Cholesky" | custom-call | tf_op jit(solution)/shard_map/cholesky/custom-call.1 | solution.py:53
  195.1 9.8 %custom-call.11 = f32[1,128,128]{1,2,0:T(8,128)S(1)} custom-call(f32[1,128,128]{2,1,0:T(8,128)S(1)} %fusion.7), custom_call_target="InvertDiagBlocksLowerTriangular" | custom-call | tf_op jit(solution)/shard_map/triangular_solve/custom-call.0 | solution.py:54
  204.9 3.7 %all-to-all-start.5 = ((f32[16,64,384]{2,1,0:T(8,128)}), f32[16,64,384]{2,1,0:T(8,128)S(1)}, u32[]{:S(2)}, u32[]{:S(2)}) async-start(f32[16,64,384]{2,1,0:T(8,128)} %bitcast.4), calls=%async_computation.5 | async-start | bytes 3145728 | tf_op jit(solution)/shard_map/all_to_all | solution.py:13
  212.8 12.5 %custom-call.12 = f32[128,128]{1,0:T(8,128)S(1)} custom-call(f32[128,128]{1,0:T(8,128)} %convolution_subtract_fusion.3), custom_call_target="Cholesky" | custom-call | tf_op jit(solution)/shard_map/cholesky/custom-call.1 | solution.py:53
  227.3 11.3 %custom-call.13 = f32[1,128,128]{1,2,0:T(8,128)} custom-call(f32[1,128,128]{2,1,0:T(8,128)} %fusion.8), custom_call_target="InvertDiagBlocksLowerTriangular" | custom-call | tf_op jit(solution)/shard_map/triangular_solve/custom-call.0 | solution.py:54
  243.5 7.4 %all-to-all-start.6 = ((f32[16,64,384]{2,1,0:T(8,128)}), f32[16,64,384]{2,1,0:T(8,128)S(1)}, u32[]{:S(2)}, u32[]{:S(2)}) async-start(f32[16,64,384]{2,1,0:T(8,128)} %broadcast_in_dim.11), calls=%async_computation.6 | async-start | bytes 3145728 | tf_op jit(solution)/shard_map/all_to_all | solution.py:21
  254.1 11.7 %custom-call.14 = f32[128,128]{1,0:T(8,128)S(1)} custom-call(f32[128,128]{1,0:T(8,128)S(1)} %convolution_subtract_fusion), custom_call_target="Cholesky" | custom-call | tf_op jit(solution)/shard_map/cholesky/custom-call.1 | solution.py:53
  267.0 9.8 %custom-call.15 = f32[1,128,128]{1,2,0:T(8,128)S(1)} custom-call(f32[1,128,128]{2,1,0:T(8,128)S(1)} %fusion.9), custom_call_target="InvertDiagBlocksLowerTriangular" | custom-call | tf_op jit(solution)/shard_map/triangular_solve/custom-call.0 | solution.py:54
  277.1 3.1 all-to-all-done.6
  280.2 33.8 %all-reduce.3.cloned.1.call-done = (f32[384,1848]{0,1:T(8,128)}, f32[768,48]{1,0:T(8,128)}) async-done(((f32[384,1848]{0,1:T(8,128)}, f32[768,48]{1,0:T(8,128)}), (f32[384,1848]{0,1:T(8,128)}, f32[768,48]{1,0:T(8,128)})) %all-reduce.3.cloned.1.call-update) | async-done | bytes 2986000 | tf_op jit(solution)/shard_map/psum | solution.py:91
  (84 shorter events, 39.1 us)
Async XLA Ops:
  7.2 87.0 %copy-start = (bf16[768,1848]{0,1:T(8,128)(2,1)S(1)}, bf16[768,1848]{0,1:T(8,128)(2,1)}, u32[]{:S(2)}) copy-start(bf16[768,1848]{0,1:T(8,128)(2,1)} %param.14) | copy-start | bytes 8515588
  7.2 201.7 %reduce-scatter.4.cloned.1.call-start = ((), (), s32[]{:S(2)}) async-start(), calls=%async_computation.8 | async-start | bytes 2506752
  7.2 2.2 copy-start.2
  81.4 5.8 %copy-start.12 = (bf16[1848,384]{1,0:T(8,128)(2,1)S(1)}, bf16[1848,384]{1,0:T(8,128)(2,1)}, u32[]{:S(2)}) copy-start(bf16[1848,384]{1,0:T(8,128)(2,1)} %param.11) | copy-start | bytes 4257796
  87.2 3.5 %copy-start.4 = (bf16[1024,1848]{0,1:T(8,128)(2,1)}, bf16[1024,1848]{0,1:T(8,128)(2,1)S(1)}, u32[]{:S(2)}) copy-start(bf16[1024,1848]{0,1:T(8,128)(2,1)S(1)} %subtract_convert_fusion) | copy-start | bytes 11354116
  87.2 3.5 %copy-start.9 = (bf16[768,1024]{1,0:T(8,128)(2,1)S(1)}, bf16[768,1024]{1,0:T(8,128)(2,1)}, u32[]{:S(2)}) copy-start(bf16[768,1024]{1,0:T(8,128)(2,1)} %param.13) | copy-start | bytes 4718596
  132.1 26.6 %copy-start.13 = (bf16[384,1024]{1,0:T(8,128)(2,1)S(1)}, bf16[384,1024]{1,0:T(8,128)(2,1)}, u32[]{:S(2)}) copy-start(bf16[384,1024]{1,0:T(8,128)(2,1)} %param.12) | copy-start | bytes 2359300
  154.6 25.1 %all-to-all-start.4 = ((f32[16,48,384]{2,1,0:T(8,128)}), f32[16,48,384]{2,1,0:T(8,128)S(1)}, u32[]{:S(2)}, u32[]{:S(2)}) async-start(f32[16,48,384]{2,1,0:T(8,128)} %broadcast_in_dim.10), calls=%async_computation.4 | async-start | bytes 2359296 | tf_op jit(solution)/shard_map/all_to_all | solution.py:21
  204.9 35.7 %all-to-all-start.5 = ((f32[16,64,384]{2,1,0:T(8,128)}), f32[16,64,384]{2,1,0:T(8,128)S(1)}, u32[]{:S(2)}, u32[]{:S(2)}) async-start(f32[16,64,384]{2,1,0:T(8,128)} %bitcast.4), calls=%async_computation.5 | async-start | bytes 3145728 | tf_op jit(solution)/shard_map/all_to_all | solution.py:13
  208.6 105.4 %all-reduce.3.cloned.1.call-start = ((), (), s32[]{:S(2)}) async-start(), calls=%async_computation.9 | async-start | bytes 6463488 | tf_op jit(solution)/shard_map/psum | solution.py:91
  211.0 0.6 copy-start.6
  243.5 36.7 %all-to-all-start.6 = ((f32[16,64,384]{2,1,0:T(8,128)}), f32[16,64,384]{2,1,0:T(8,128)S(1)}, u32[]{:S(2)}, u32[]{:S(2)}) async-start(f32[16,64,384]{2,1,0:T(8,128)} %broadcast_in_dim.11), calls=%async_computation.6 | async-start | bytes 3145728 | tf_op jit(solution)/shard_map/all_to_all | solution.py:21
  252.0 1.4 copy-start.10
  253.2 0.6 copy-start.7
  254.0 66.1 %copy-start.8 = (f32[128,128]{1,0:T(8,128)S(1)}, f32[128,128]{1,0:T(8,128)}, u32[]{:S(2)}) copy-start(f32[128,128]{1,0:T(8,128)} %copy-done.7) | copy-start | bytes 196612
  254.1 66.3 %copy-start.11 = (f32[128,128]{1,0:T(8,128)S(1)}, f32[128,128]{1,0:T(8,128)}, u32[]{:S(2)}) copy-start(f32[128,128]{1,0:T(8,128)} %copy-done.10) | copy-start | bytes 196612
  280.2 35.9 %copy-start.3 = (f32[16,64,384]{2,1,0:T(8,128)}, f32[16,64,384]{2,1,0:T(8,128)S(1)}, u32[]{:S(2)}) copy-start(f32[16,64,384]{2,1,0:T(8,128)S(1)} %all-to-all-done.6) | copy-start | bytes 4718596
  314.0 11.4 %copy-start.5 = (f32[384,1848]{0,1:T(8,128)S(1)}, f32[384,1848]{0,1:T(8,128)}, u32[]{:S(2)}) copy-start(f32[384,1848]{0,1:T(8,128)} %get-tuple-element.15) | copy-start | bytes 8515588
  322.6 4.4 %copy-start.1 = (bf16[768,1848]{0,1:T(8,128)(2,1)S(1)}, bf16[768,1848]{0,1:T(8,128)(2,1)}, u32[]{:S(2)}) copy-start(bf16[768,1848]{0,1:T(8,128)(2,1)} %param.14) | copy-start | bytes 8515588
Sparse Core Ops, SparseCore 0:
  104.0 74.6 reduce-scatter.3
  212.6 101.3 all-reduce.2

commit v6 on v3

--- a/solution.py
+++ b/solution.py
@@ -67,12 +67,13 @@
     difference = (adjusted_block.astype(jnp.float32) - base_weight.astype(jnp.float32)).astype(
         jnp.bfloat16
     )
+    corange_part = jnp.dot(corange_test, difference, preferred_element_type=jnp.float32)
+    corange_sketch = lax.psum(corange_part, "row")
     left_product = jnp.dot(core_left, difference, preferred_element_type=jnp.float32)
     partial_value = jnp.dot(left_product, core_right.astype(jnp.float32).T, precision=highest)
     own_columns = lax.psum_scatter(partial_value, "col", scatter_dimension=1, tiled=True)
+    own_columns, corange_sketch = lax.optimization_barrier((own_columns, corange_sketch))
     own_columns = lax.psum(own_columns, "row")
-    corange_part = jnp.dot(corange_test, difference, preferred_element_type=jnp.float32)
-    corange_sketch = lax.psum(corange_part, "row")
     range_part = jnp.dot(difference, range_test, preferred_element_type=jnp.float32)
     left_float = core_left.astype(jnp.float32)
     projected_part = jnp.dot(left_float, range_part, precision=highest)

time: 323 us -> 408 us (1.26)
  waiting for transfers between devices: 84.3 us -> 153 us
  blocking collectives: 43.6 us -> 57 us
    psum x0 -> x1, waiting for transfers between devices: none -> 71.7 us  [local(): own_columns = lax.psum(own_columns, 'row')]
    psum x1, waiting for transfers between devices: 26.4 us -> 0.02 us  [local(): corange_sketch = lax.psum(corange_part, 'row')]
    all_to_all x2, waiting for transfers between devices: 15.5 us -> 38.6 us  [gather_rows(): return lax.all_to_all(tiled, axis, split_axis=0, concat_axis=0, tiled=True)]
    all_to_all x2, blocking collectives: 34.8 us -> 48 us  [scatter_sum(): got = lax.all_to_all(part, axis, split_axis=0, concat_axis=0, tiled=True)]
    unnamed x1 -> x0, matrix products: 9.62 us -> none
    dot_general x0 -> x1, matrix products: none -> 9.42 us  [local(): jnp.dot(left_product, core_right.astype(jnp.float32).T, precision=highest)]
    unnamed x34 -> x15, local copies, waits for them, and re-layouts: 14.7 us -> 11.4 us
  transfers between devices with their start and end apart: 6 -> 7, of which waited for: 4 -> 4; matrix products, arithmetic and copies ran while one was open for 34% -> 30% of each run, Pallas kernels for 0% -> 0%
where the time goes in v6:
time: 408 us; the launch traced here: 403 us
  waiting for transfers between devices  153 us (38%)
  other arithmetic  77.7 us (19%)
  blocking collectives  57 us (14%)
  matrix products  44.7 us (11%)
  local copies, waits for them, and re-layouts  31.2 us (8%)
  starting transfers between devices  24 us (6%)
  between operations  16 us (4%)
    psum x1, waiting for transfers between devices, local(): own_columns = lax.psum(own_columns, 'row')  71.7 us
    all_to_all x2, blocking collectives, scatter_sum(): got = lax.all_to_all(part, axis, split_axis=0, concat_axis=0, tiled=True)  48 us
    all_to_all x1, waiting for transfers between devices, local(): lax.all_to_all(by_target, 'col', split_axis=0, concat_axis=0, tiled=True)  42.3 us
    all_to_all x2, waiting for transfers between devices, gather_rows(): return lax.all_to_all(tiled, axis, split_axis=0, concat_axis=0, tiled=True)  38.6 us
    another operation x9, other arithmetic, cholesky_solve(): low[j, j] = lax.linalg.cholesky(a, symmetrize_input=False)  37.3 us
    another operation x6, other arithmetic, cholesky_solve(): lax.linalg.triangular_solve(low[j, j], eye, left_side=True, lower=True)  31.4 us
    reshape x2, local copies, waits for them, and re-layouts, local(): by_target = adjusted_rows.reshape(height, ncol, width).transpose(1, 0, 2)  13.5 us
    unnamed x15, local copies, waits for them, and re-layouts  11.4 us
  transfers between devices with their start and end apart: 7, of which 4 were waited for; matrix products, arithmetic and copies ran while one was open for 30% of the time, Pallas kernels for 0%

profile of v6, /device:TPU:0, one launch (start us, length us, event | category | flops | bytes accessed | tf_op | source)
XLA Modules:
  0.0 403.3 jit_solution(6987794893904349774)
XLA Ops:
  8.0 8.6 %reshape.50 = bf16[64,16,1848]{2,1,0:T(8,128)(2,1)} reshape(bf16[64,29568]{1,0:T(8,128)(2,1)} %param.9) | data formatting | bytes 7569408 | tf_op jit(solution)/shard_map/reshape | solution.py:64
  16.6 4.9 %copy.16 = bf16[64,16,1848]{2,0,1:T(8,128)(2,1)} copy(bf16[64,16,1848]{2,1,0:T(8,128)(2,1)} %reshape.50) | data formatting | bytes 7569408 | tf_op jit(solution)/shard_map/reshape | solution.py:64
  21.5 7.2 %all-to-all-start = ((bf16[16,64,1848]{2,1,0:T(8,128)(2,1)}), bf16[16,64,1848]{2,1,0:T(8,128)(2,1)}, u32[]{:S(2)}, u32[]{:S(2)}) async-start(bf16[16,64,1848]{2,1,0:T(8,128)(2,1)} %bitcast.82), calls=%async_computation | async-start | bytes 7864320 | tf_op jit(solution)/shard_map/all_to_all | solution.py:65
  29.2 6.2 %copy.12 = bf16[1024,1848]{1,0:T(8,128)(2,1)} copy(bf16[1024,1848]{0,1:T(8,128)(2,1)} %param.10) | data formatting | bytes 7569408 | tf_op args[1]
  35.3 42.3 %all-to-all-done = bf16[16,64,1848]{2,1,0:T(8,128)(2,1)} async-done(((bf16[16,64,1848]{2,1,0:T(8,128)(2,1)}), bf16[16,64,1848]{2,1,0:T(8,128)(2,1)}, u32[]{:S(2)}, u32[]{:S(2)}) %all-to-all-start) | async-done | bytes 3784736 | tf_op jit(solution)/shard_map/all_to_all | solution.py:65
  77.7 4.4 %fusion = bf16[1024,1848]{1,0:T(8,128)(2,1)S(1)} fusion(bf16[1024,1848]{1,0:T(8,128)(2,1)} %copy.12, bf16[16,64,1848]{2,1,0:T(8,128)(2,1)} %all-to-all-done), kind=kLoop, calls=%fused_computation.1 | loop fusion | flops 7569408 | bytes 11354112 | tf_op jit(solution)/shard_map/convert_element_type | solution.py:67
  89.3 6.9 %convolution_bitcast_fusion.1 = f32[768,384]{0,1:T(8,128)} fusion(f32[1024,384]{1,0:T(8,128)} %fusion.20, bf16[768,1024]{1,0:T(8,128)(2,1)} %param.13), kind=kOutput, calls=%fused_computation.4 | convolution fusion | flops 3623878656 | bytes 4325376 | tf_op jit(solution)/shard_map/dot_general | solution.py:79
  98.9 36.6 %all_to_all.56 = f32[16,48,384]{2,1,0:T(8,128)} all-to-all(f32[16,48,384]{2,1,0:T(8,128)} %bitcast.84), channel_id=1, replica_groups=mesh['row'=8,'col'=16] {'col'}, dimensions={0} | all-to-all | bytes 2359296 | tf_op jit(solution)/shard_map/all_to_all | solution.py:11
  136.9 11.4 %all_to_all.57 = f32[8,6,384]{2,1,0:T(8,128)S(1)} all-to-all(f32[8,6,384]{2,1,0:T(8,128)S(1)} %all_to_all.40), channel_id=1, replica_groups=mesh['row'=8,'col'=16] {'row'}, dimensions={0} | all-to-all | bytes 147456 | tf_op jit(solution)/shard_map/all_to_all | solution.py:11
  148.3 9.0 %all_to_all.58 = f32[8,6,384]{2,1,0:T(8,128)S(1)} all-to-all(f32[8,6,384]{2,1,0:T(8,128)S(1)} %broadcast_in_dim.8), channel_id=1, replica_groups=mesh['row'=8,'col'=16] {'row'}, dimensions={0} | all-to-all | bytes 147456 | tf_op jit(solution)/shard_map/all_to_all | solution.py:19
  158.6 4.4 %all-to-all-start.4 = ((f32[16,48,384]{2,1,0:T(8,128)}), f32[16,48,384]{2,1,0:T(8,128)}, u32[]{:S(2)}, u32[]{:S(2)}) async-start(f32[16,48,384]{2,1,0:T(8,128)} %broadcast_in_dim.10), calls=%async_computation.4 | async-start | bytes 2359296 | tf_op jit(solution)/shard_map/all_to_all | solution.py:19
  163.2 6.1 %fusion.21 = f32[1848,768]{1,0:T(8,128)S(1)} fusion(bf16[1024,1848]{1,0:T(8,128)(2,1)} %copy-done.1, bf16[768,1024]{1,0:T(8,128)(2,1)} %param.13), kind=kOutput, calls=%fused_computation.48 | convolution fusion | flops 2906652672 | bytes 11034624 | tf_op jit(solution)/shard_map/dot_general | solution.py:72
  169.3 9.4 %fusion.22 = f32[768,768]{0,1:T(8,128)} fusion(f32[1848,768]{1,0:T(8,128)S(1)} %fusion.21, bf16[768,1848]{0,1:T(8,128)(2,1)S(1)} %copy-done), kind=kOutput, calls=%fused_computation.49 | convolution fusion | flops 13079937024 | bytes 10874880 | tf_op jit(solution)/shard_map/dot_general | solution.py:73
  178.7 16.7 %all-to-all-done.4 = f32[16,48,384]{2,1,0:T(8,128)} async-done(((f32[16,48,384]{2,1,0:T(8,128)}), f32[16,48,384]{2,1,0:T(8,128)}, u32[]{:S(2)}, u32[]{:S(2)}) %all-to-all-start.4) | async-done | bytes 1179680 | tf_op jit(solution)/shard_map/all_to_all | solution.py:19
  195.4 4.4 %all-to-all-start.5 = ((f32[16,64,384]{2,1,0:T(8,128)}), f32[16,64,384]{2,1,0:T(8,128)}, u32[]{:S(2)}, u32[]{:S(2)}) async-start(f32[16,64,384]{2,1,0:T(8,128)} %bitcast.83), calls=%async_computation.5 | async-start | bytes 3145728 | tf_op jit(solution)/shard_map/all_to_all | solution.py:11
  207.1 11.7 %custom-call.10 = f32[128,128]{1,0:T(8,128)S(1)} custom-call(f32[128,128]{1,0:T(8,128)S(1)} %slice.40), custom_call_target="Cholesky" | custom-call | tf_op jit(solution)/shard_map/cholesky/custom-call.1 | solution.py:37
  220.1 9.8 %custom-call.11 = f32[1,128,128]{1,2,0:T(8,128)S(1)} custom-call(f32[1,128,128]{2,1,0:T(8,128)S(1)} %fusion.8), custom_call_target="InvertDiagBlocksLowerTriangular" | custom-call | tf_op jit(solution)/shard_map/triangular_solve/custom-call.0 | solution.py:38
  232.5 11.9 %custom-call.12 = f32[128,128]{1,0:T(8,128)S(1)} custom-call(f32[128,128]{1,0:T(8,128)S(1)} %convolution_subtract_fusion.3), custom_call_target="Cholesky" | custom-call | tf_op jit(solution)/shard_map/cholesky/custom-call.1 | solution.py:37
  245.7 9.8 %custom-call.13 = f32[1,128,128]{1,2,0:T(8,128)S(1)} custom-call(f32[1,128,128]{2,1,0:T(8,128)S(1)} %fusion.9), custom_call_target="InvertDiagBlocksLowerTriangular" | custom-call | tf_op jit(solution)/shard_map/triangular_solve/custom-call.0 | solution.py:38
  259.6 11.7 %custom-call.14 = f32[128,128]{1,0:T(8,128)S(1)} custom-call(f32[128,128]{1,0:T(8,128)S(1)} %convolution_subtract_fusion), custom_call_target="Cholesky" | custom-call | tf_op jit(solution)/shard_map/cholesky/custom-call.1 | solution.py:37
  272.7 9.8 %custom-call.15 = f32[1,128,128]{1,2,0:T(8,128)S(1)} custom-call(f32[1,128,128]{2,1,0:T(8,128)S(1)} %fusion.10), custom_call_target="InvertDiagBlocksLowerTriangular" | custom-call | tf_op jit(solution)/shard_map/triangular_solve/custom-call.0 | solution.py:38
  282.9 71.7 %all-reduce.5.cloned.1.call-done = f32[768,48]{0,1:T(8,128)} async-done(((f32[768,48]{0,1:T(8,128)}), f32[768,48]{0,1:T(8,128)}) %all-reduce.5.cloned.1.call-update) | async-done | bytes 147472 | tf_op jit(solution)/shard_map/psum | solution.py:76
  360.8 6.8 %all-to-all-start.6 = ((f32[16,64,384]{2,1,0:T(8,128)}), f32[16,64,384]{2,1,0:T(8,128)}, u32[]{:S(2)}, u32[]{:S(2)}) async-start(f32[16,64,384]{2,1,0:T(8,128)} %broadcast_in_dim.11), calls=%async_computation.6 | async-start | bytes 3145728 | tf_op jit(solution)/shard_map/all_to_all | solution.py:19
  369.5 21.9 %all-to-all-done.6 = f32[16,64,384]{2,1,0:T(8,128)} async-done(((f32[16,64,384]{2,1,0:T(8,128)}), f32[16,64,384]{2,1,0:T(8,128)}, u32[]{:S(2)}, u32[]{:S(2)}) %all-to-all-start.6) | async-done | bytes 1572896 | tf_op jit(solution)/shard_map/all_to_all | solution.py:19
  (71 shorter events, 43.9 us)
Async XLA Ops:
  8.0 161.3 %copy-start = (bf16[768,1848]{0,1:T(8,128)(2,1)S(1)}, bf16[768,1848]{0,1:T(8,128)(2,1)}, u32[]{:S(2)}) copy-start(bf16[768,1848]{0,1:T(8,128)(2,1)} %param.14) | copy-start | bytes 8515588
  21.5 56.2 %all-to-all-start = ((bf16[16,64,1848]{2,1,0:T(8,128)(2,1)}), bf16[16,64,1848]{2,1,0:T(8,128)(2,1)}, u32[]{:S(2)}, u32[]{:S(2)}) async-start(bf16[16,64,1848]{2,1,0:T(8,128)(2,1)} %bitcast.82), calls=%async_computation | async-start | bytes 7864320 | tf_op jit(solution)/shard_map/all_to_all | solution.py:65
  28.7 253.9 %all-reduce.3.cloned.1.call-start = ((), (), s32[]{:S(2)}) async-start(), calls=%async_computation.9 | async-start | bytes 5677056 | tf_op jit(solution)/shard_map/psum | solution.py:71
  77.7 4.4 %copy-start.4 = (bf16[1848,384]{1,0:T(8,128)(2,1)S(1)}, bf16[1848,384]{1,0:T(8,128)(2,1)}, u32[]{:S(2)}) copy-start(bf16[1848,384]{1,0:T(8,128)(2,1)} %param.11) | copy-start | bytes 4257796
  82.1 3.4 copy-start.1
  82.1 3.4 copy-start.5
  158.6 36.8 %all-to-all-start.4 = ((f32[16,48,384]{2,1,0:T(8,128)}), f32[16,48,384]{2,1,0:T(8,128)}, u32[]{:S(2)}, u32[]{:S(2)}) async-start(f32[16,48,384]{2,1,0:T(8,128)} %broadcast_in_dim.10), calls=%async_computation.4 | async-start | bytes 2359296 | tf_op jit(solution)/shard_map/all_to_all | solution.py:19
  163.0 119.6 %reduce-scatter.2.cloned.1.call-start = ((), (), s32[]{:S(2)}) async-start(), calls=%async_computation.8 | async-start | bytes 2506752 | tf_op jit(solution)/shard_map/reduce_scatter | solution.py:74
  195.4 162.6 %all-to-all-start.5 = ((f32[16,64,384]{2,1,0:T(8,128)}), f32[16,64,384]{2,1,0:T(8,128)}, u32[]{:S(2)}, u32[]{:S(2)}) async-start(f32[16,64,384]{2,1,0:T(8,128)} %bitcast.83), calls=%async_computation.5 | async-start | bytes 3145728 | tf_op jit(solution)/shard_map/all_to_all | solution.py:11
  199.8 154.8 %all-reduce.5.cloned.1.call-start = ((), (), s32[]{:S(2)}) async-start(), calls=%async_computation.10 | async-start | bytes 294912 | tf_op jit(solution)/shard_map/psum | solution.py:76
  206.2 0.9 copy-start.3
  360.8 30.5 %all-to-all-start.6 = ((f32[16,64,384]{2,1,0:T(8,128)}), f32[16,64,384]{2,1,0:T(8,128)}, u32[]{:S(2)}, u32[]{:S(2)}) async-start(f32[16,64,384]{2,1,0:T(8,128)} %broadcast_in_dim.11), calls=%async_computation.6 | async-start | bytes 3145728 | tf_op jit(solution)/shard_map/all_to_all | solution.py:19
  391.4 2.8 copy-start.2
Sparse Core Ops, SparseCore 0:
  89.4 109.0 all-reduce.2
  282.7 71.8 all-reduce.4
Sparse Core Ops, SparseCore 1:
  178.8 76.3 reduce-scatter.1

commit v7 on v3

--- a/solution.py
+++ b/solution.py
@@ -17,6 +17,15 @@
         groups * chunk.shape[0], *chunk.shape[1:]
     )
     return lax.all_to_all(tiled, axis, split_axis=0, concat_axis=0, tiled=True)
+
+
+def dot_exact(wide, narrow):
+    high = wide.astype(jnp.bfloat16)
+    rest = wide - high.astype(jnp.float32)
+    middle = rest.astype(jnp.bfloat16)
+    low = (rest - middle.astype(jnp.float32)).astype(jnp.bfloat16)
+    out = [jnp.dot(piece, narrow, preferred_element_type=jnp.float32) for piece in (high, middle, low)]
+    return out[0] + (out[1] + out[2])
 
 
 def dot_hi(a, b):
@@ -68,7 +77,7 @@
         jnp.bfloat16
     )
     left_product = jnp.dot(core_left, difference, preferred_element_type=jnp.float32)
-    partial_value = jnp.dot(left_product, core_right.astype(jnp.float32).T, precision=highest)
+    partial_value = dot_exact(left_product, core_right.T)
     own_columns = lax.psum_scatter(partial_value, "col", scatter_dimension=1, tiled=True)
     own_columns = lax.psum(own_columns, "row")
     corange_part = jnp.dot(corange_test, difference, preferred_element_type=jnp.float32)

time: 323 us -> 326 us (level)
    dot_general x0 -> x3, matrix products: none -> 10.2 us  [dot_exact(): jnp.dot(piece, narrow, preferred_element_type=jnp.float32)]
    unnamed x1 -> x0, matrix products: 9.62 us -> none
  transfers between devices with their start and end apart: 6 -> 6, of which waited for: 4 -> 4; matrix products, arithmetic and copies ran while one was open for 34% -> 33% of each run, Pallas kernels for 0% -> 0%
where the time goes in v7:
time: 326 us; the launch traced here: 321 us
  waiting for transfers between devices  84.3 us (26%)
  other arithmetic  78.5 us (24%)
  matrix products  45.2 us (14%)
  blocking collectives  43.6 us (13%)
  local copies, waits for them, and re-layouts  32.9 us (10%)
  starting transfers between devices  22 us (7%)
  between operations  14.9 us (5%)
    all_to_all x1, waiting for transfers between devices, local(): lax.all_to_all(by_target, 'col', split_axis=0, concat_axis=0, tiled=True)  42.3 us
    another operation x9, other arithmetic, cholesky_solve(): low[j, j] = lax.linalg.cholesky(a, symmetrize_input=False)  38.2 us
    all_to_all x2, blocking collectives, scatter_sum(): got = lax.all_to_all(part, axis, split_axis=0, concat_axis=0, tiled=True)  34.8 us
    another operation x6, other arithmetic, cholesky_solve(): lax.linalg.triangular_solve(low[j, j], eye, left_side=True, lower=True)  33.4 us
    psum x1, waiting for transfers between devices, local(): corange_sketch = lax.psum(corange_part, 'row')  26.2 us
    all_to_all x2, waiting for transfers between devices, gather_rows(): return lax.all_to_all(tiled, axis, split_axis=0, concat_axis=0, tiled=True)  15.7 us
    unnamed x34, local copies, waits for them, and re-layouts  14.7 us
    reshape x2, local copies, waits for them, and re-layouts, local(): by_target = adjusted_rows.reshape(height, ncol, width).transpose(1, 0, 2)  13.5 us
  transfers between devices with their start and end apart: 6, of which 4 were waited for; matrix products, arithmetic and copies ran while one was open for 33% of the time, Pallas kernels for 0%

profile of v7, /device:TPU:0, one launch (start us, length us, event | category | flops | bytes accessed | tf_op | source)
XLA Modules:
  0.0 321.4 jit_solution(2605216757773161312)
XLA Ops:
  7.2 8.6 %reshape.50 = bf16[64,16,1848]{2,1,0:T(8,128)(2,1)} reshape(bf16[64,29568]{1,0:T(8,128)(2,1)} %param.9) | data formatting | bytes 7569408 | tf_op jit(solution)/shard_map/reshape | solution.py:73
  15.8 4.9 %copy.23 = bf16[64,16,1848]{2,0,1:T(8,128)(2,1)} copy(bf16[64,16,1848]{2,1,0:T(8,128)(2,1)} %reshape.50) | data formatting | bytes 7569408 | tf_op jit(solution)/shard_map/reshape | solution.py:73
  20.6 7.2 %all-to-all-start = ((bf16[16,64,1848]{2,1,0:T(8,128)(2,1)}), bf16[16,64,1848]{2,1,0:T(8,128)(2,1)}, u32[]{:S(2)}, u32[]{:S(2)}) async-start(bf16[16,64,1848]{2,1,0:T(8,128)(2,1)} %bitcast.115), calls=%async_computation | async-start | bytes 7864320 | tf_op jit(solution)/shard_map/all_to_all | solution.py:74
  27.9 6.6 %copy.16 = bf16[1024,1848]{1,0:T(8,128)(2,1)} copy(bf16[1024,1848]{0,1:T(8,128)(2,1)} %param.10) | data formatting | bytes 7569408 | tf_op args[1]
  34.5 42.3 %all-to-all-done = bf16[16,64,1848]{2,1,0:T(8,128)(2,1)} async-done(((bf16[16,64,1848]{2,1,0:T(8,128)(2,1)}), bf16[16,64,1848]{2,1,0:T(8,128)(2,1)}, u32[]{:S(2)}, u32[]{:S(2)}) %all-to-all-start) | async-done | bytes 3784736 | tf_op jit(solution)/shard_map/all_to_all | solution.py:74
  76.8 4.4 %fusion = bf16[1024,1848]{1,0:T(8,128)(2,1)S(1)} fusion(bf16[1024,1848]{1,0:T(8,128)(2,1)} %copy.16, bf16[16,64,1848]{2,1,0:T(8,128)(2,1)} %all-to-all-done), kind=kLoop, calls=%fused_computation.1 | loop fusion | flops 7569408 | bytes 11354112 | tf_op jit(solution)/shard_map/convert_element_type | solution.py:76
  81.2 3.5 %fusion.31 = f32[1848,768]{1,0:T(8,128)S(1)} fusion(bf16[1024,1848]{1,0:T(8,128)(2,1)S(1)} %fusion, bf16[768,1024]{1,0:T(8,128)(2,1)S(1)} %copy-done.10), kind=kOutput, calls=%fused_computation.59 | convolution fusion | flops 2906652672 | bytes 11034624 | tf_op jit(solution)/shard_map/dot_general | solution.py:79
  93.8 4.6 %add_bitcast_fusion = f32[768,768]{1,0:T(8,128)} fusion(f32[768,768]{0,1:T(8,128)S(1)} %fusion.26, f32[768,768]{0,1:T(8,128)S(1)} %fusion.3, bf16[768,1848]{0,1:T(8,128)(2,1)S(1)} %copy-done, f32[1848,768]{1,0:T(8,128)S(1)} %fusion.31), kind=kOutput, calls=%fused_computation.11 | convolution fusion | flops 2191104000 | bytes 15593472 | tf_op jit(solution)/shard_map/dot_general | solution.py:27
  98.4 5.8 %convolution_bitcast_fusion.1 = f32[768,384]{0,1:T(8,128)S(1)} fusion(f32[1024,384]{1,0:T(8,128)} %fusion.29, bf16[768,1024]{1,0:T(8,128)(2,1)} %param.13), kind=kOutput, calls=%fused_computation.12 | convolution fusion | flops 3623878656 | bytes 4325376 | tf_op jit(solution)/shard_map/dot_general | solution.py:87
  104.6 22.4 %all_to_all.56 = f32[16,48,384]{2,1,0:T(8,128)S(1)} all-to-all(f32[16,48,384]{2,1,0:T(8,128)S(1)} %bitcast.117), channel_id=1, replica_groups=mesh['row'=8,'col'=16] {'col'}, dimensions={0} | all-to-all | bytes 2359296 | tf_op jit(solution)/shard_map/all_to_all | solution.py:11
  127.0 12.4 %all_to_all.57 = f32[8,6,384]{2,1,0:T(8,128)S(1)} all-to-all(f32[8,6,384]{2,1,0:T(8,128)S(1)} %all_to_all.40), channel_id=1, replica_groups=mesh['row'=8,'col'=16] {'row'}, dimensions={0} | all-to-all | bytes 147456 | tf_op jit(solution)/shard_map/all_to_all | solution.py:11
  139.5 8.8 %all_to_all.58 = f32[8,6,384]{2,1,0:T(8,128)S(1)} all-to-all(f32[8,6,384]{2,1,0:T(8,128)S(1)} %broadcast_in_dim.8), channel_id=1, replica_groups=mesh['row'=8,'col'=16] {'row'}, dimensions={0} | all-to-all | bytes 147456 | tf_op jit(solution)/shard_map/all_to_all | solution.py:19
  149.4 3.7 %all-to-all-start.4 = ((f32[16,48,384]{2,1,0:T(8,128)}), f32[16,48,384]{2,1,0:T(8,128)S(1)}, u32[]{:S(2)}, u32[]{:S(2)}) async-start(f32[16,48,384]{2,1,0:T(8,128)} %broadcast_in_dim.10), calls=%async_computation.4 | async-start | bytes 2359296 | tf_op jit(solution)/shard_map/all_to_all | solution.py:19
  153.1 5.9 %convolution_bitcast_fusion = f32[384,1848]{0,1:T(8,128)} fusion(bf16[1024,1848]{1,0:T(8,128)(2,1)} %copy-done.3, bf16[384,1024]{1,0:T(8,128)(2,1)S(1)} %copy-done.14), kind=kOutput, calls=%fused_computation.9 | convolution fusion | flops 1453326336 | bytes 7409664 | tf_op jit(solution)/shard_map/dot_general | solution.py:83
  159.1 15.0 %all-to-all-done.4 = f32[16,48,384]{2,1,0:T(8,128)S(1)} async-done(((f32[16,48,384]{2,1,0:T(8,128)}), f32[16,48,384]{2,1,0:T(8,128)S(1)}, u32[]{:S(2)}, u32[]{:S(2)}) %all-to-all-start.4) | async-done | bytes 1179680 | tf_op jit(solution)/shard_map/all_to_all | solution.py:19
  174.1 3.7 %all-to-all-start.5 = ((f32[16,64,384]{2,1,0:T(8,128)}), f32[16,64,384]{2,1,0:T(8,128)S(1)}, u32[]{:S(2)}, u32[]{:S(2)}) async-start(f32[16,64,384]{2,1,0:T(8,128)} %bitcast.5), calls=%async_computation.5 | async-start | bytes 3145728 | tf_op jit(solution)/shard_map/all_to_all | solution.py:11
  183.1 11.7 %custom-call.10 = f32[128,128]{1,0:T(8,128)S(1)} custom-call(f32[128,128]{1,0:T(8,128)S(1)} %slice.40), custom_call_target="Cholesky" | custom-call | tf_op jit(solution)/shard_map/cholesky/custom-call.1 | solution.py:46
  196.2 9.8 %custom-call.11 = f32[1,128,128]{1,2,0:T(8,128)S(1)} custom-call(f32[1,128,128]{2,1,0:T(8,128)S(1)} %fusion.13), custom_call_target="InvertDiagBlocksLowerTriangular" | custom-call | tf_op jit(solution)/shard_map/triangular_solve/custom-call.0 | solution.py:47
  210.0 12.8 %custom-call.12 = f32[128,128]{1,0:T(8,128)S(1)} custom-call(f32[128,128]{1,0:T(8,128)} %convolution_subtract_fusion.3), custom_call_target="Cholesky" | custom-call | tf_op jit(solution)/shard_map/cholesky/custom-call.1 | solution.py:46
  224.8 11.3 %custom-call.13 = f32[1,128,128]{1,2,0:T(8,128)} custom-call(f32[1,128,128]{2,1,0:T(8,128)} %fusion.14), custom_call_target="InvertDiagBlocksLowerTriangular" | custom-call | tf_op jit(solution)/shard_map/triangular_solve/custom-call.0 | solution.py:47
  240.9 7.2 %all-to-all-start.6 = ((f32[16,64,384]{2,1,0:T(8,128)}), f32[16,64,384]{2,1,0:T(8,128)S(1)}, u32[]{:S(2)}, u32[]{:S(2)}) async-start(f32[16,64,384]{2,1,0:T(8,128)} %broadcast_in_dim.11), calls=%async_computation.6 | async-start | bytes 3145728 | tf_op jit(solution)/shard_map/all_to_all | solution.py:19
  251.3 11.7 %custom-call.14 = f32[128,128]{1,0:T(8,128)S(1)} custom-call(f32[128,128]{1,0:T(8,128)S(1)} %convolution_subtract_fusion), custom_call_target="Cholesky" | custom-call | tf_op jit(solution)/shard_map/cholesky/custom-call.1 | solution.py:46
  264.2 9.8 %custom-call.15 = f32[1,128,128]{1,2,0:T(8,128)S(1)} custom-call(f32[1,128,128]{2,1,0:T(8,128)S(1)} %fusion.15), custom_call_target="InvertDiagBlocksLowerTriangular" | custom-call | tf_op jit(solution)/shard_map/triangular_solve/custom-call.0 | solution.py:47
  275.0 26.2 %all-reduce.3.cloned.1.call-done = (f32[384,1848]{0,1:T(8,128)}, f32[768,48]{1,0:T(8,128)}) async-done(((f32[384,1848]{0,1:T(8,128)}, f32[768,48]{1,0:T(8,128)}), (f32[384,1848]{0,1:T(8,128)}, f32[768,48]{1,0:T(8,128)})) %all-reduce.3.cloned.1.call-update) | async-done | bytes 2986000 | tf_op jit(solution)/shard_map/psum | solution.py:84
  (89 shorter events, 46.4 us)
Async XLA Ops:
  7.2 77.5 %copy-start = (bf16[768,1848]{0,1:T(8,128)(2,1)S(1)}, bf16[768,1848]{0,1:T(8,128)(2,1)}, u32[]{:S(2)}) copy-start(bf16[768,1848]{0,1:T(8,128)(2,1)} %param.14) | copy-start | bytes 8515588
  20.6 56.2 %all-to-all-start = ((bf16[16,64,1848]{2,1,0:T(8,128)(2,1)}), bf16[16,64,1848]{2,1,0:T(8,128)(2,1)}, u32[]{:S(2)}, u32[]{:S(2)}) async-start(bf16[16,64,1848]{2,1,0:T(8,128)(2,1)} %bitcast.115), calls=%async_computation | async-start | bytes 7864320 | tf_op jit(solution)/shard_map/all_to_all | solution.py:74
  27.8 178.2 %reduce-scatter.4.cloned.1.call-start = ((), (), s32[]{:S(2)}) async-start(), calls=%async_computation.8 | async-start | bytes 2506752
  76.8 4.4 %copy-start.10 = (bf16[768,1024]{1,0:T(8,128)(2,1)S(1)}, bf16[768,1024]{1,0:T(8,128)(2,1)}, u32[]{:S(2)}) copy-start(bf16[768,1024]{1,0:T(8,128)(2,1)} %param.13) | copy-start | bytes 4718596
  81.2 9.2 %copy-start.3 = (bf16[1024,1848]{1,0:T(8,128)(2,1)}, bf16[1024,1848]{1,0:T(8,128)(2,1)S(1)}, u32[]{:S(2)}) copy-start(bf16[1024,1848]{1,0:T(8,128)(2,1)S(1)} %fusion) | copy-start | bytes 11354116
  87.6 2.9 copy-start.13
  127.0 26.2 %copy-start.14 = (bf16[384,1024]{1,0:T(8,128)(2,1)S(1)}, bf16[384,1024]{1,0:T(8,128)(2,1)}, u32[]{:S(2)}) copy-start(bf16[384,1024]{1,0:T(8,128)(2,1)} %param.12) | copy-start | bytes 2359300
  149.4 24.7 %all-to-all-start.4 = ((f32[16,48,384]{2,1,0:T(8,128)}), f32[16,48,384]{2,1,0:T(8,128)S(1)}, u32[]{:S(2)}, u32[]{:S(2)}) async-start(f32[16,48,384]{2,1,0:T(8,128)} %broadcast_in_dim.10), calls=%async_computation.4 | async-start | bytes 2359296 | tf_op jit(solution)/shard_map/all_to_all | solution.py:19
  174.1 64.0 %all-to-all-start.5 = ((f32[16,64,384]{2,1,0:T(8,128)}), f32[16,64,384]{2,1,0:T(8,128)S(1)}, u32[]{:S(2)}, u32[]{:S(2)}) async-start(f32[16,64,384]{2,1,0:T(8,128)} %bitcast.5), calls=%async_computation.5 | async-start | bytes 3145728 | tf_op jit(solution)/shard_map/all_to_all | solution.py:11
  177.8 123.3 %all-reduce.3.cloned.1.call-start = ((), (), s32[]{:S(2)}) async-start(), calls=%async_computation.9 | async-start | bytes 6463488 | tf_op jit(solution)/shard_map/psum | solution.py:84
  182.3 0.8 copy-start.5
  183.1 25.7 %copy-start.6 = (f32[384,384]{1,0:T(8,128)S(1)}, f32[384,384]{1,0:T(8,128)}, u32[]{:S(2)}) copy-start(f32[384,384]{1,0:T(8,128)} %copy-done.5) | copy-start | bytes 1769476
  208.2 0.6 copy-start.7
  240.9 34.0 %all-to-all-start.6 = ((f32[16,64,384]{2,1,0:T(8,128)}), f32[16,64,384]{2,1,0:T(8,128)S(1)}, u32[]{:S(2)}, u32[]{:S(2)}) async-start(f32[16,64,384]{2,1,0:T(8,128)} %broadcast_in_dim.11), calls=%async_computation.6 | async-start | bytes 3145728 | tf_op jit(solution)/shard_map/all_to_all | solution.py:19
  249.2 1.4 copy-start.11
  250.4 0.6 copy-start.8
  251.3 56.1 %copy-start.9 = (f32[128,128]{1,0:T(8,128)S(1)}, f32[128,128]{1,0:T(8,128)}, u32[]{:S(2)}) copy-start(f32[128,128]{1,0:T(8,128)} %copy-done.8) | copy-start | bytes 196612
  251.3 56.3 %copy-start.12 = (f32[128,128]{1,0:T(8,128)S(1)}, f32[128,128]{1,0:T(8,128)}, u32[]{:S(2)}) copy-start(f32[128,128]{1,0:T(8,128)} %copy-done.11) | copy-start | bytes 196612
  275.0 28.3 %copy-start.2 = (f32[16,64,384]{2,1,0:T(8,128)}, f32[16,64,384]{2,1,0:T(8,128)S(1)}, u32[]{:S(2)}) copy-start(f32[16,64,384]{2,1,0:T(8,128)S(1)} %all-to-all-done.6) | copy-start | bytes 4718596
  301.1 11.4 %copy-start.4 = (f32[384,1848]{0,1:T(8,128)S(1)}, f32[384,1848]{0,1:T(8,128)}, u32[]{:S(2)}) copy-start(f32[384,1848]{0,1:T(8,128)} %get-tuple-element.15) | copy-start | bytes 8515588
  309.7 4.4 %copy-start.1 = (bf16[768,1848]{0,1:T(8,128)(2,1)S(1)}, bf16[768,1848]{0,1:T(8,128)(2,1)}, u32[]{:S(2)}) copy-start(bf16[768,1848]{0,1:T(8,128)(2,1)} %param.14) | copy-start | bytes 8515588
Sparse Core Ops, SparseCore 0:
  98.5 76.5 reduce-scatter.3
  208.0 93.0 all-reduce.2
